TPU v7x, 512 devices: a whole 4x4x16 slice. The times are simulated.
512 devices in a mesh: clus: 128 (over x, z, core), sub: 4 (over y).
Axes of the slice: x: 4, y: 4, z: 16, core: 2. Of those that a mesh axis runs over, the one named last changes fastest.
Arguments:
- residual_in: float32 [2048, 32, 512], P(('clus', 'sub')), may hold values from -6 to 6
- local_inverse: bfloat16 [2048, 512, 512], P(('clus', 'sub')), may hold values from -3 to 3
- coarse_basis: float32 [2048, 8, 512], P(('clus', 'sub')), may hold values from -0.6 to 0.6
- level2_inverse: float32 [128, 128, 128], P('clus'), may hold values from -3 to 3
- level2_basis: float32 [128, 32, 128], P('clus'), may hold values from -1.5 to 1.5
- level3_inverse: float32 [4096, 4096], P('clus'), may hold values from -3 to 3
Outputs:
- preconditioned: float32 [2048, 32, 512], P(('clus', 'sub'))
All inputs are finite; a program needn't handle non-finite values.
Results may differ from a plain program's by a relative error of at most 0.00084.
Values sent between devices are 32-bit elements; how exact they have to be, the bound alone decides.
No kernel may reach another device: no remote copies, remote signals or barrier semaphores. Data moves between devices by JAX's collectives and lax.ppermute only.
A program may use at most 64 MiB of HBM per device.

v0:
```python
import jax
import jax.numpy as jnp
from jax import lax
from jax.sharding import PartitionSpec as P

IFW = 128


def from_behind_2(array, axis, by):
    count = lax.axis_size(axis)
    pairs = [(i, i + by) for i in range(count) if 0 <= i + by < count]
    return lax.ppermute(array, axis, pairs)


def couple(values_in):
    lower_rim = values_in[:, :, :IFW]
    upper_rim = values_in[:, :, values_in.shape[2] - IFW :]
    from_before = from_behind_2(upper_rim[-1:], ("clus", "sub"), 1)
    from_behind = from_behind_2(lower_rim[:1], ("clus", "sub"), -1)
    prev_rims = jnp.concatenate([from_before, upper_rim[:-1]], 0)
    next_rims = jnp.concatenate([lower_rim[1:], from_behind], 0)
    coupled = values_in.at[:, :, :IFW].add(0.5 * prev_rims)
    return coupled.at[:, :, values_in.shape[2] - IFW :].add(0.5 * next_rims)


def shards(residual_in, local_inverse, coarse_basis, level2_inverse, level2_basis, level3_inverse):
    high = lax.Precision.HIGHEST
    rhs = couple(residual_in)
    rhs_low = rhs.astype(jnp.bfloat16)
    local = jnp.einsum("srk,sjk->srj", rhs_low, local_inverse, preferred_element_type=jnp.float32)
    coarse = jnp.einsum("snk,srk->snr", coarse_basis, rhs, precision=high)
    gathered = lax.all_gather(coarse, "sub", axis=0, tiled=True)
    groups = gathered.reshape(-1, gathered.shape[2])
    level2 = jnp.dot(level2_inverse[0], groups, precision=high)
    level3_in = jnp.dot(level2_basis[0], groups, precision=high)
    position = lax.axis_index("sub")
    level3 = jnp.dot(
        level3_inverse, lax.all_gather(level3_in, "clus", axis=0, tiled=True), precision=high
    )
    corrected = level2 + jnp.dot(level2_basis[0].T, level3, precision=high)
    own_count = coarse.shape[0] * coarse.shape[1]
    own_rows = lax.dynamic_slice_in_dim(corrected, position * own_count, own_count, 0)
    per_sub = own_rows.reshape(coarse.shape[0], coarse.shape[1], -1)
    update = local + jnp.einsum("snk,snr->srk", coarse_basis, per_sub, precision=high)
    return couple(update)


def solution(mesh):
    in_specs = (
        P(("clus", "sub"), None, None),
        P(("clus", "sub"), None, None),
        P(("clus", "sub"), None, None),
        P("clus", None, None),
        P("clus", None, None),
        P("clus", None),
    )
    out_specs = P(("clus", "sub"), None, None)
    return jax.shard_map(shards, mesh=mesh, in_specs=in_specs, out_specs=out_specs, check_vma=False)
```

profile of v0, /device:TPU:24, one launch (start us, length us, event | category | flops | bytes accessed | tf_op | source)
XLA Modules:
  0.0 154.9 jit_solution(14654597493924026100)
XLA Ops:
  0.0 0.0 copy-start
  0.0 1.1 copy.16
  1.1 2.6 %collective-permute-start.1 = (f32[1,32,128]{2,1,0:T(8,128)S(1)}, f32[1,32,128]{2,1,0:T(8,128)S(1)}, u32[]{:S(2)}, u32[]{:S(2)}) collective-permute-start(f32[1,32,128]{2,1,0:T(8,128)S(1)} %get-tuple-element.59), channel_id=1, source_target_pairs={{1,0},{2,1},{3,2},{4,3},{5,4},{6,5},{7,6},{8,7},{9,8},{10,9},{11,1... | collective-permute-start | bytes 49160 | tf_op jit(solution)/shard_map/ppermute | solution.py:12
  3.8 4.1 %collective-permute-start = (f32[1,32,128]{2,1,0:T(8,128)S(1)}, f32[1,32,128]{2,1,0:T(8,128)S(1)}, u32[]{:S(2)}, u32[]{:S(2)}) collective-permute-start(f32[1,32,128]{2,1,0:T(8,128)S(1)} %get-tuple-element.60), channel_id=1, source_target_pairs={{0,1},{1,2},{2,3},{3,4},{4,5},{5,6},{6,7},{7,8},{8,9},{9,10},{10,1... | collective-permute-start | bytes 49160 | tf_op jit(solution)/shard_map/ppermute | solution.py:12
  7.9 1.5 collective-permute-done
  9.4 0.0 collective-permute-done.1
  9.5 1.2 convolution_bitcast_fusion.1
  10.6 15.5 %all_gather.6 = f32[16,8,32]{2,1,0:T(8,128)S(1)} all-gather(f32[4,8,32]{2,1,0:T(8,128)S(1)} %convolution_bitcast_fusion.1), channel_id=1, replica_groups=mesh['clus'=128,'sub'=4] {'sub'}, dimensions={0}, use_global_device_ids=true | all-gather | bytes 20480 | tf_op jit(solution)/shard_map/all_gather | solution.py:32
  26.1 0.9 convolution_bitcast_fusion
  27.1 1.1 fusion.6
  28.2 0.1 copy.9
  28.3 108.7 %all_gather.7 = f32[4096,32]{1,0:T(8,128)S(1)} all-gather(f32[32,32]{1,0:T(8,128)S(1)} %copy.9), channel_id=1, replica_groups=mesh['clus'=128,'sub'=4] {'clus'}, dimensions={0}, use_global_device_ids=true | all-gather | bytes 528384 | tf_op jit(solution)/shard_map/all_gather | solution.py:38
  137.0 3.4 %fusion.20 = f32[32,32]{1,0:T(8,128)S(1)} fusion(f32[4096,32]{1,0:T(8,128)S(1)} %all_gather.7, f32[32,4096]{1,0:T(8,128)S(1)} %copy-done.2), kind=kOutput, calls=%fused_computation.31 | convolution fusion | flops 50331648 | bytes 1052672 | tf_op jit(solution)/shard_map/dot_general | solution.py:37
  140.4 0.1 fusion.13
  140.5 0.1 fusion.10
  140.6 0.1 copy.10
  140.7 0.4 fusion.11
  141.2 0.7 convolution_add_fusion
  141.9 5.1 %collective-permute-start.2 = (f32[1,32,128]{2,1,0:T(8,128)S(1)}, f32[1,32,128]{2,1,0:T(8,128)S(1)}, u32[]{:S(2)}, u32[]{:S(2)}) collective-permute-start(f32[1,32,128]{2,1,0:T(8,128)S(1)} %get-tuple-element.56), channel_id=1, source_target_pairs={{0,1},{1,2},{2,3},{3,4},{4,5},{5,6},{6,7},{7,8},{8,9},{9,10},{10,1... | collective-permute-start | bytes 49160 | tf_op jit(solution)/shard_map/ppermute | solution.py:12
  147.0 1.9 %collective-permute-start.3 = (f32[1,32,128]{2,1,0:T(8,128)S(1)}, f32[1,32,128]{2,1,0:T(8,128)S(1)}, u32[]{:S(2)}, u32[]{:S(2)}) collective-permute-start(f32[1,32,128]{2,1,0:T(8,128)S(1)} %get-tuple-element.55), channel_id=1, source_target_pairs={{1,0},{2,1},{3,2},{4,3},{5,4},{6,5},{7,6},{8,7},{9,8},{10,9},{11,1... | collective-permute-start | bytes 49160 | tf_op jit(solution)/shard_map/ppermute | solution.py:12
  148.9 0.0 collective-permute-done.2
  149.0 0.0 copy-start.1
  149.0 4.5 %collective-permute-done.3 = f32[1,32,128]{2,1,0:T(8,128)S(1)} collective-permute-done((f32[1,32,128]{2,1,0:T(8,128)S(1)}, f32[1,32,128]{2,1,0:T(8,128)S(1)}, u32[]{:S(2)}, u32[]{:S(2)}) %collective-permute-start.3) | collective-permute-done | bytes 16416 | tf_op jit(solution)/shard_map/ppermute | solution.py:12
  153.5 1.5 fusion.1
  (15 shorter events, 0.1 us)
Async XLA Ops:
  0.0 141.2 %copy-start = (bf16[4,512,512]{2,1,0:T(8,128)(2,1)S(1)}, bf16[4,512,512]{2,1,0:T(8,128)(2,1)}, u32[]{:S(2)}) copy-start(bf16[4,512,512]{2,1,0:T(8,128)(2,1)} %param.15) | copy-start | bytes 6291460
  0.0 137.0 %copy-start.2 = (f32[32,4096]{1,0:T(8,128)S(1)}, f32[32,4096]{1,0:T(8,128)}, u32[]{:S(2)}) copy-start(f32[32,4096]{1,0:T(8,128)} %param.19) | copy-start | bytes 1572868
  1.1 8.3 %collective-permute-start.1 = (f32[1,32,128]{2,1,0:T(8,128)S(1)}, f32[1,32,128]{2,1,0:T(8,128)S(1)}, u32[]{:S(2)}, u32[]{:S(2)}) collective-permute-start(f32[1,32,128]{2,1,0:T(8,128)S(1)} %get-tuple-element.59), channel_id=1, source_target_pairs={{1,0},{2,1},{3,2},{4,3},{5,4},{6,5},{7,6},{8,7},{9,8},{10,9},{11,1... | collective-permute-start | bytes 49160 | tf_op jit(solution)/shard_map/ppermute | solution.py:12
  3.8 5.6 %collective-permute-start = (f32[1,32,128]{2,1,0:T(8,128)S(1)}, f32[1,32,128]{2,1,0:T(8,128)S(1)}, u32[]{:S(2)}, u32[]{:S(2)}) collective-permute-start(f32[1,32,128]{2,1,0:T(8,128)S(1)} %get-tuple-element.60), channel_id=1, source_target_pairs={{0,1},{1,2},{2,3},{3,4},{4,5},{5,6},{6,7},{7,8},{8,9},{9,10},{10,1... | collective-permute-start | bytes 49160 | tf_op jit(solution)/shard_map/ppermute | solution.py:12
  28.3 112.1 %copy-start.4 = (f32[1,32,128]{2,1,0:T(8,128)S(1)}, f32[1,32,128]{2,1,0:T(8,128)}, u32[]{:S(2)}) copy-start(f32[1,32,128]{2,1,0:T(8,128)} %param.18) | copy-start | bytes 49156
  28.3 112.4 %copy-start.3 = (f32[4,8,512]{2,1,0:T(8,128)S(1)}, f32[4,8,512]{2,1,0:T(8,128)}, u32[]{:S(2)}) copy-start(f32[4,8,512]{2,1,0:T(8,128)} %param.16) | copy-start | bytes 196612
  141.9 7.0 %collective-permute-start.2 = (f32[1,32,128]{2,1,0:T(8,128)S(1)}, f32[1,32,128]{2,1,0:T(8,128)S(1)}, u32[]{:S(2)}, u32[]{:S(2)}) collective-permute-start(f32[1,32,128]{2,1,0:T(8,128)S(1)} %get-tuple-element.56), channel_id=1, source_target_pairs={{0,1},{1,2},{2,3},{3,4},{4,5},{5,6},{6,7},{7,8},{8,9},{9,10},{10,1... | collective-permute-start | bytes 49160 | tf_op jit(solution)/shard_map/ppermute | solution.py:12
  147.0 6.4 %collective-permute-start.3 = (f32[1,32,128]{2,1,0:T(8,128)S(1)}, f32[1,32,128]{2,1,0:T(8,128)S(1)}, u32[]{:S(2)}, u32[]{:S(2)}) collective-permute-start(f32[1,32,128]{2,1,0:T(8,128)S(1)} %get-tuple-element.55), channel_id=1, source_target_pairs={{1,0},{2,1},{3,2},{4,3},{5,4},{6,5},{7,6},{8,7},{9,8},{10,9},{11,1... | collective-permute-start | bytes 49160 | tf_op jit(solution)/shard_map/ppermute | solution.py:12
  149.0 4.5 %copy-start.1 = (f32[4,32,512]{2,1,0:T(8,128)}, f32[4,32,512]{2,1,0:T(8,128)S(1)}, u32[]{:S(2)}) copy-start(f32[4,32,512]{2,1,0:T(8,128)S(1)} %fusion.2) | copy-start | bytes 786436
where the time goes:
time: 157 us; the launch traced here: 155 us
  blocking collectives  124 us (79%)
  starting transfers between devices  13.8 us (9%)
  matrix products  7.85 us (5%)
  waiting for transfers between devices  5.95 us (4%)
  other arithmetic  1.63 us (1%)
    all_gather x1, blocking collectives, shards(): lax.all_gather(level3_in, 'clus', axis=0, tiled=True)  109 us
    all_gather x1, blocking collectives, shards(): gathered = lax.all_gather(coarse, 'sub', axis=0, tiled=True)  15.5 us
    ppermute x4, starting transfers between devices, from_behind_2(): return lax.ppermute(array, axis, pairs)  13.8 us
    ppermute x4, waiting for transfers between devices, from_behind_2(): return lax.ppermute(array, axis, pairs)  5.95 us
    dot_general x1, matrix products, shards(): jnp.dot(level3_inverse, lax.all_gather(level3_in, 'clus', axis=0, tiled=T...  3.38 us
  transfers between devices with their start and end apart: 4, of which 2 were waited for; matrix products, arithmetic and copies ran while one was open for 0% of the time, Pallas kernels for 0%

commit v1 on v0

--- a/solution.py
+++ b/solution.py
@@ -1,7 +1,7 @@
 import jax
 import jax.numpy as jnp
 from jax import lax
-from jax.sharding import PartitionSpec as P
+from jax.sharding import Mesh, PartitionSpec as P
 
 IFW = 128
 
@@ -15,8 +15,8 @@
 def couple(values_in):
     lower_rim = values_in[:, :, :IFW]
     upper_rim = values_in[:, :, values_in.shape[2] - IFW :]
-    from_before = from_behind_2(upper_rim[-1:], ("clus", "sub"), 1)
-    from_behind = from_behind_2(lower_rim[:1], ("clus", "sub"), -1)
+    from_before = from_behind_2(upper_rim[-1:], ("x", "z", "core", "sub"), 1)
+    from_behind = from_behind_2(lower_rim[:1], ("x", "z", "core", "sub"), -1)
     prev_rims = jnp.concatenate([from_before, upper_rim[:-1]], 0)
     next_rims = jnp.concatenate([lower_rim[1:], from_behind], 0)
     coupled = values_in.at[:, :, :IFW].add(0.5 * prev_rims)
@@ -34,9 +34,10 @@
     level2 = jnp.dot(level2_inverse[0], groups, precision=high)
     level3_in = jnp.dot(level2_basis[0], groups, precision=high)
     position = lax.axis_index("sub")
-    level3 = jnp.dot(
-        level3_inverse, lax.all_gather(level3_in, "clus", axis=0, tiled=True), precision=high
-    )
+    gathered_in = level3_in
+    for axis in ("core", "z", "x"):
+        gathered_in = lax.all_gather(gathered_in, axis, axis=0, tiled=True)
+    level3 = jnp.dot(level3_inverse, gathered_in, precision=high)
     corrected = level2 + jnp.dot(level2_basis[0].T, level3, precision=high)
     own_count = coarse.shape[0] * coarse.shape[1]
     own_rows = lax.dynamic_slice_in_dim(corrected, position * own_count, own_count, 0)
@@ -46,13 +47,19 @@
 
 
 def solution(mesh):
+    clus, sub = mesh.shape["clus"], mesh.shape["sub"]
+    x_size = 4
+    z_size = clus // (2 * x_size)
+    split = Mesh(mesh.devices.reshape(x_size, z_size, 2, sub), ("x", "z", "core", "sub"))
+    clus_axes = ("x", "z", "core")
+    spread = (*clus_axes, "sub")
     in_specs = (
-        P(("clus", "sub"), None, None),
-        P(("clus", "sub"), None, None),
-        P(("clus", "sub"), None, None),
-        P("clus", None, None),
-        P("clus", None, None),
-        P("clus", None),
+        P(spread, None, None),
+        P(spread, None, None),
+        P(spread, None, None),
+        P(clus_axes, None, None),
+        P(clus_axes, None, None),
+        P(clus_axes, None),
     )
-    out_specs = P(("clus", "sub"), None, None)
-    return jax.shard_map(shards, mesh=mesh, in_specs=in_specs, out_specs=out_specs, check_vma=False)
+    out_specs = P(spread, None, None)
+    return jax.shard_map(shards, mesh=split, in_specs=in_specs, out_specs=out_specs, check_vma=False)

time: 157 us -> 96.9 us (0.62)
  the two profiles are of different devices: /device:TPU:24 before, /device:TPU:2 now
where the time goes in v1:
time: 96.9 us; the launch traced here: 96.4 us
  blocking collectives  54.2 us (56%)
  starting transfers between devices  25 us (26%)
  waiting for transfers between devices  8.69 us (9%)
  matrix products  5.04 us (5%)
  local copies, waits for them, and re-layouts  1.7 us (2%)
  other arithmetic  1.62 us (2%)
    all_gather x3, blocking collectives, shards(): gathered_in = lax.all_gather(gathered_in, axis, axis=0, tiled=True)  42.4 us
    ppermute x4, starting transfers between devices, from_behind_2(): return lax.ppermute(array, axis, pairs)  25 us
    all_gather x1, blocking collectives, shards(): gathered = lax.all_gather(coarse, 'sub', axis=0, tiled=True)  11.9 us
    ppermute x4, waiting for transfers between devices, from_behind_2(): return lax.ppermute(array, axis, pairs)  8.69 us
  transfers between devices with their start and end apart: 4, of which 2 were waited for; matrix products, arithmetic and copies ran while one was open for 0% of the time, Pallas kernels for 0%

profile of v1, /device:TPU:2, one launch (start us, length us, event | category | flops | bytes accessed | tf_op | source)
XLA Modules:
  0.0 96.4 jit_solution(16763550646034404233)
XLA Ops:
  0.0 1.1 %copy.19 = f32[4,32,512]{2,1,0:T(8,128)S(1)} copy(f32[4,32,512]{2,1,0:T(8,128)} %param.14) | data formatting | bytes 524288
  1.1 13.3 %collective-permute-start.1 = (f32[1,32,128]{2,1,0:T(8,128)S(1)}, f32[1,32,128]{2,1,0:T(8,128)S(1)}, u32[]{:S(2)}, u32[]{:S(2)}) collective-permute-start(f32[1,32,128]{2,1,0:T(8,128)S(1)} %get-tuple-element.59), channel_id=1, source_target_pairs={{1,0},{2,1},{3,2},{4,3},{5,4},{6,5},{7,6},{8,7},{9,8},{10,9},{11,1... | collective-permute-start | bytes 49160 | tf_op jit(solution)/shard_map/ppermute | solution.py:12
  14.4 1.9 %collective-permute-start = (f32[1,32,128]{2,1,0:T(8,128)S(1)}, f32[1,32,128]{2,1,0:T(8,128)S(1)}, u32[]{:S(2)}, u32[]{:S(2)}) collective-permute-start(f32[1,32,128]{2,1,0:T(8,128)S(1)} %get-tuple-element.60), channel_id=1, source_target_pairs={{0,1},{1,2},{2,3},{3,4},{4,5},{5,6},{6,7},{7,8},{8,9},{9,10},{10,1... | collective-permute-start | bytes 49160 | tf_op jit(solution)/shard_map/ppermute | solution.py:12
  16.3 7.3 %collective-permute-done = f32[1,32,128]{2,1,0:T(8,128)S(1)} collective-permute-done((f32[1,32,128]{2,1,0:T(8,128)S(1)}, f32[1,32,128]{2,1,0:T(8,128)S(1)}, u32[]{:S(2)}, u32[]{:S(2)}) %collective-permute-start) | collective-permute-done | bytes 16416 | tf_op jit(solution)/shard_map/ppermute | solution.py:12
  23.7 1.2 %convolution_bitcast_fusion.1 = f32[4,8,32]{2,1,0:T(8,128)S(1)} fusion(f32[4,32,512]{2,1,0:T(8,128)S(1)} %fusion.3, f32[4,8,512]{2,1,0:T(8,128)} %param.16), kind=kOutput, calls=%fused_computation.2 | convolution fusion | flops 6291456 | bytes 331776 | tf_op jit(solution)/shard_map/snk,srk->snr/dot_general | solution.py:31
  24.9 11.9 %all_gather.12 = f32[16,8,32]{2,1,0:T(8,128)S(1)} all-gather(f32[4,8,32]{2,1,0:T(8,128)S(1)} %convolution_bitcast_fusion.1), channel_id=1, replica_groups=mesh['x'=4,'z'=16,'core'=2,'sub'=4] {'sub'}, dimensions={0}, use_global_device_ids=true | all-gather | bytes 20480 | tf_op jit(solution)/shard_map/all_gather | solution.py:32
  36.8 0.9 convolution_bitcast_fusion
  37.7 1.1 %fusion.6 = f32[32,128]{1,0:T(8,128)S(1)} fusion(f32[1,128,128]{2,1,0:T(8,128)} %param.17, f32[16,8,32]{2,1,0:T(8,128)S(1)} %all_gather.12), kind=kOutput, calls=%fused_computation.16 | convolution fusion | flops 6291456 | bytes 98304 | tf_op jit(solution)/shard_map/dot_general | solution.py:34
  38.8 0.1 copy.10
  38.9 1.8 %all_gather.13 = f32[64,32]{1,0:T(8,128)S(1)} all-gather(f32[32,32]{1,0:T(8,128)S(1)} %copy.10), channel_id=1, replica_groups=mesh['x'=4,'z'=16,'core'=2,'sub'=4] {'core'}, dimensions={0}, use_global_device_ids=true | all-gather | bytes 12288 | tf_op jit(solution)/shard_map/all_gather | solution.py:39
  40.8 27.4 %all-gather = f32[16,64,32]{1,2,0:T(8,128)S(1)} all-gather(f32[1,64,32]{1,2,0:T(8,128)S(1)} %copy.11), channel_id=1, replica_groups=mesh['x'=4,'z'=16,'core'=2,'sub'=4] {'z'}, dimensions={0}, use_global_device_ids=true | all-gather | bytes 139264 | tf_op jit(solution)/shard_map/all_gather | solution.py:39
  68.2 0.2 copy.12
  68.4 0.1 reshape.125
  68.5 13.1 %all_gather.15 = f32[4096,32]{0,1:T(8,128)S(1)} all-gather(f32[1024,32]{0,1:T(8,128)S(1)} %reshape.125), channel_id=1, replica_groups=mesh['x'=4,'z'=16,'core'=2,'sub'=4] {'x'}, dimensions={0}, use_global_device_ids=true | all-gather | bytes 655360 | tf_op jit(solution)/shard_map/all_gather | solution.py:39
  81.6 0.6 fusion.20
  82.2 0.1 fusion.13
  82.3 0.1 fusion.10
  82.4 0.1 copy.13
  82.5 0.4 fusion.11
  83.0 0.7 convolution_add_fusion
  83.7 1.9 %collective-permute-start.2 = (f32[1,32,128]{2,1,0:T(8,128)S(1)}, f32[1,32,128]{2,1,0:T(8,128)S(1)}, u32[]{:S(2)}, u32[]{:S(2)}) collective-permute-start(f32[1,32,128]{2,1,0:T(8,128)S(1)} %get-tuple-element.56), channel_id=1, source_target_pairs={{0,1},{1,2},{2,3},{3,4},{4,5},{5,6},{6,7},{7,8},{8,9},{9,10},{10,1... | collective-permute-start | bytes 49160 | tf_op jit(solution)/shard_map/ppermute | solution.py:12
  85.7 7.9 %collective-permute-start.3 = (f32[1,32,128]{2,1,0:T(8,128)S(1)}, f32[1,32,128]{2,1,0:T(8,128)S(1)}, u32[]{:S(2)}, u32[]{:S(2)}) collective-permute-start(f32[1,32,128]{2,1,0:T(8,128)S(1)} %get-tuple-element.55), channel_id=1, source_target_pairs={{1,0},{2,1},{3,2},{4,3},{5,4},{6,5},{7,6},{8,7},{9,8},{10,9},{11,1... | collective-permute-start | bytes 49160 | tf_op jit(solution)/shard_map/ppermute | solution.py:12
  93.6 1.4 %collective-permute-done.3 = f32[1,32,128]{2,1,0:T(8,128)S(1)} collective-permute-done((f32[1,32,128]{2,1,0:T(8,128)S(1)}, f32[1,32,128]{2,1,0:T(8,128)S(1)}, u32[]{:S(2)}, u32[]{:S(2)}) %collective-permute-start.3) | collective-permute-done | bytes 16416 | tf_op jit(solution)/shard_map/ppermute | solution.py:12
  95.0 1.5 %fusion.1 = f32[4,32,512]{2,1,0:T(8,128)} fusion(f32[4,32,512]{2,1,0:T(8,128)} %copy-done.1, f32[1,32,128]{2,1,0:T(8,128)S(1)} %collective-permute-done.3, f32[3,32,128]{2,1,0:T(8,128)S(1)} %get-tuple-element.53), kind=kLoop, calls=%fused_computation.5 | loop fusion | flops 49152 | bytes 196608 | tf_op jit(solution)/shard_map/scatter-add | solution.py:23
  (20 shorter events, 0.2 us)
Async XLA Ops:
  0.0 83.0 %copy-start = (bf16[4,512,512]{2,1,0:T(8,128)(2,1)S(1)}, bf16[4,512,512]{2,1,0:T(8,128)(2,1)}, u32[]{:S(2)}) copy-start(bf16[4,512,512]{2,1,0:T(8,128)(2,1)} %param.15) | copy-start | bytes 6291460
  0.0 81.6 %copy-start.2 = (f32[32,4096]{1,0:T(8,128)S(1)}, f32[32,4096]{1,0:T(8,128)}, u32[]{:S(2)}) copy-start(f32[32,4096]{1,0:T(8,128)} %param.19) | copy-start | bytes 1572868
  1.1 22.6 %collective-permute-start.1 = (f32[1,32,128]{2,1,0:T(8,128)S(1)}, f32[1,32,128]{2,1,0:T(8,128)S(1)}, u32[]{:S(2)}, u32[]{:S(2)}) collective-permute-start(f32[1,32,128]{2,1,0:T(8,128)S(1)} %get-tuple-element.59), channel_id=1, source_target_pairs={{1,0},{2,1},{3,2},{4,3},{5,4},{6,5},{7,6},{8,7},{9,8},{10,9},{11,1... | collective-permute-start | bytes 49160 | tf_op jit(solution)/shard_map/ppermute | solution.py:12
  14.4 9.3 %collective-permute-start = (f32[1,32,128]{2,1,0:T(8,128)S(1)}, f32[1,32,128]{2,1,0:T(8,128)S(1)}, u32[]{:S(2)}, u32[]{:S(2)}) collective-permute-start(f32[1,32,128]{2,1,0:T(8,128)S(1)} %get-tuple-element.60), channel_id=1, source_target_pairs={{0,1},{1,2},{2,3},{3,4},{4,5},{5,6},{6,7},{7,8},{8,9},{9,10},{10,1... | collective-permute-start | bytes 49160 | tf_op jit(solution)/shard_map/ppermute | solution.py:12
  16.3 65.9 %copy-start.4 = (f32[1,32,128]{2,1,0:T(8,128)S(1)}, f32[1,32,128]{2,1,0:T(8,128)}, u32[]{:S(2)}) copy-start(f32[1,32,128]{2,1,0:T(8,128)} %param.18) | copy-start | bytes 49156
  23.7 58.9 %copy-start.3 = (f32[4,8,512]{2,1,0:T(8,128)S(1)}, f32[4,8,512]{2,1,0:T(8,128)}, u32[]{:S(2)}) copy-start(f32[4,8,512]{2,1,0:T(8,128)} %param.16) | copy-start | bytes 196612
  83.7 9.8 %collective-permute-start.2 = (f32[1,32,128]{2,1,0:T(8,128)S(1)}, f32[1,32,128]{2,1,0:T(8,128)S(1)}, u32[]{:S(2)}, u32[]{:S(2)}) collective-permute-start(f32[1,32,128]{2,1,0:T(8,128)S(1)} %get-tuple-element.56), channel_id=1, source_target_pairs={{0,1},{1,2},{2,3},{3,4},{4,5},{5,6},{6,7},{7,8},{8,9},{9,10},{10,1... | collective-permute-start | bytes 49160 | tf_op jit(solution)/shard_map/ppermute | solution.py:12
  85.7 9.3 %collective-permute-start.3 = (f32[1,32,128]{2,1,0:T(8,128)S(1)}, f32[1,32,128]{2,1,0:T(8,128)S(1)}, u32[]{:S(2)}, u32[]{:S(2)}) collective-permute-start(f32[1,32,128]{2,1,0:T(8,128)S(1)} %get-tuple-element.55), channel_id=1, source_target_pairs={{1,0},{2,1},{3,2},{4,3},{5,4},{6,5},{7,6},{8,7},{9,8},{10,9},{11,1... | collective-permute-start | bytes 49160 | tf_op jit(solution)/shard_map/ppermute | solution.py:12
  93.6 1.4 %copy-start.1 = (f32[4,32,512]{2,1,0:T(8,128)}, f32[4,32,512]{2,1,0:T(8,128)S(1)}, u32[]{:S(2)}) copy-start(f32[4,32,512]{2,1,0:T(8,128)S(1)} %fusion.2) | copy-start | bytes 786436

commit v2 on v1

v2 whole, which is shorter than its diff:
```python
import jax
import jax.numpy as jnp
from jax import lax
from jax.sharding import Mesh, PartitionSpec as P

IFW = 128
SPREAD = ("x", "z", "core", "sub")


def from_behind_2(array, axis, by, only=None):
    count = lax.axis_size(axis)
    pairs = [(i, i + by) for i in range(count) if 0 <= i + by < count and (only is None or only(i))]
    return lax.ppermute(array, axis, pairs)


def couple(values_in):
    lower_rim = values_in[:, :, :IFW]
    upper_rim = values_in[:, :, values_in.shape[2] - IFW :]
    from_before = from_behind_2(upper_rim[-1:], SPREAD, 1)
    from_behind = from_behind_2(lower_rim[:1], SPREAD, -1)
    return add_rims(values_in, from_before, from_behind)


def add_rims(values_in, from_before, from_behind):
    lower_rim = values_in[:, :, :IFW]
    upper_rim = values_in[:, :, values_in.shape[2] - IFW :]
    prev_rims = jnp.concatenate([from_before, upper_rim[:-1]], 0)
    next_rims = jnp.concatenate([lower_rim[1:], from_behind], 0)
    coupled = values_in.at[:, :, :IFW].add(0.5 * prev_rims)
    return coupled.at[:, :, values_in.shape[2] - IFW :].add(0.5 * next_rims)


def rim_update(local_rim, basis_rim, coefficients):
    high = lax.Precision.HIGHEST
    return local_rim + jnp.einsum("snk,snr->srk", basis_rim, coefficients[None], precision=high)


def shards(residual_in, local_inverse, coarse_basis, level2_inverse, level2_basis, level3_inverse):
    high = lax.Precision.HIGHEST
    sub = lax.axis_size("sub")
    position = lax.axis_index("sub")
    nloc = residual_in.shape[2]
    nc = coarse_basis.shape[1]
    rhs = couple(residual_in)
    rhs_low = rhs.astype(jnp.bfloat16)
    local = jnp.einsum("srk,sjk->srj", rhs_low, local_inverse, preferred_element_type=jnp.float32)
    coarse = jnp.einsum("snk,srk->snr", coarse_basis, rhs, precision=high)
    nrhs = local.shape[1]

    first_local = local[0, :, :IFW]
    last_local = local[-1, :, nloc - IFW :]
    first_basis = coarse_basis[0, :, :IFW]
    last_basis = coarse_basis[-1, :, nloc - IFW :]
    sizes = [coarse.size, nrhs * IFW, nrhs * IFW, nc * IFW, nc * IFW]
    starts = [sum(sizes[:i]) for i in range(len(sizes) + 1)]
    packed = jnp.concatenate(
        [coarse.reshape(-1), first_local.reshape(-1), last_local.reshape(-1),
         first_basis.reshape(-1), last_basis.reshape(-1)], 0)
    gathered = lax.all_gather(packed, "sub", axis=0, tiled=False)
    groups = gathered[:, : starts[1]].reshape(-1, nrhs)
    level2 = jnp.dot(level2_inverse[0], groups, precision=high)
    level3_in = jnp.dot(level2_basis[0], groups, precision=high)

    is_last = position == sub - 1
    last_fold = jnp.dot(level2_basis[0][:, -nc:].T, level3_inverse, precision=high)
    first_fold = jnp.dot(level2_basis[0][:, :nc].T, level3_inverse, precision=high)
    to_last = jnp.concatenate(
        [last_local.reshape(-1), last_basis.reshape(-1), last_fold.reshape(-1), level2[-nc:].reshape(-1)], 0)
    to_first = jnp.concatenate(
        [first_local.reshape(-1), first_basis.reshape(-1), first_fold.reshape(-1), level2[:nc].reshape(-1)], 0)
    outgoing = jnp.where(is_last, to_last, to_first)
    count = lax.axis_size(SPREAD)
    pairs = [(i, i + 1) for i in range(sub - 1, count - 1, sub)] + [(i + 1, i) for i in range(sub - 1, count - 1, sub)]
    incoming = lax.ppermute(outgoing, SPREAD, pairs)

    gathered_in = level3_in
    for axis in ("core", "z", "x"):
        gathered_in = lax.all_gather(gathered_in, axis, axis=0, tiled=True)
    level3 = jnp.dot(level3_inverse, gathered_in, precision=high)
    corrected = level2 + jnp.dot(level2_basis[0].T, level3, precision=high)
    own_count = coarse.shape[0] * coarse.shape[1]
    own_rows = lax.dynamic_slice_in_dim(corrected, position * own_count, own_count, 0)
    per_sub = own_rows.reshape(coarse.shape[0], coarse.shape[1], -1)
    update = local + jnp.einsum("snk,snr->srk", coarse_basis, per_sub, precision=high)

    cut = [nrhs * IFW, nc * IFW, nc * level3_inverse.shape[1], nc * nrhs]
    at = [sum(cut[:i]) for i in range(len(cut) + 1)]
    cross_local = incoming[at[0] : at[1]].reshape(1, nrhs, IFW)
    cross_basis = incoming[at[1] : at[2]].reshape(1, nc, IFW)
    cross_fold = incoming[at[2] : at[3]].reshape(nc, -1)
    cross_rows = incoming[at[3] : at[4]].reshape(nc, nrhs)
    cross_coef = cross_rows + jnp.dot(cross_fold, gathered_in, precision=high)
    cross_rim = rim_update(cross_local, cross_basis, cross_coef)

    prev_device = lax.dynamic_index_in_dim(gathered, jnp.maximum(position - 1, 0), 0, keepdims=False)
    next_device = lax.dynamic_index_in_dim(gathered, jnp.minimum(position + 1, sub - 1), 0, keepdims=False)
    prev_rows = lax.dynamic_slice_in_dim(corrected, position * own_count - nc, nc, 0)
    next_rows = lax.dynamic_slice_in_dim(corrected, (position + 1) * own_count, nc, 0)
    inner_before = rim_update(
        prev_device[starts[2] : starts[3]].reshape(1, nrhs, IFW),
        prev_device[starts[4] : starts[5]].reshape(1, nc, IFW), prev_rows)
    inner_behind = rim_update(
        next_device[starts[1] : starts[2]].reshape(1, nrhs, IFW),
        next_device[starts[3] : starts[4]].reshape(1, nc, IFW), next_rows)
    from_before = jnp.where(position > 0, inner_before, cross_rim)
    from_behind = jnp.where(is_last, cross_rim, inner_behind)
    return add_rims(update, from_before, from_behind)


def solution(mesh):
    clus, sub = mesh.shape["clus"], mesh.shape["sub"]
    x_size = 4
    z_size = clus // (2 * x_size)
    split = Mesh(mesh.devices.reshape(x_size, z_size, 2, sub), SPREAD)
    clus_axes = ("x", "z", "core")
    in_specs = (
        P(SPREAD, None, None),
        P(SPREAD, None, None),
        P(SPREAD, None, None),
        P(clus_axes, None, None),
        P(clus_axes, None, None),
        P(clus_axes, None),
    )
    out_specs = P(SPREAD, None, None)
    return jax.shard_map(shards, mesh=split, in_specs=in_specs, out_specs=out_specs, check_vma=False)
```

time: 96.9 us -> 101 us (1.042)
  starting transfers between devices: 25 us -> 17.5 us
  local copies, waits for them, and re-layouts: 1.7 us -> 8.68 us
  matrix products: 5.04 us -> 11.3 us
  waiting for transfers between devices: 8.69 us -> 2.96 us
  blocking collectives: 54.2 us -> 55.9 us
  other arithmetic: 1.62 us -> 2.92 us
    ppermute x4 -> x2, starting transfers between devices: 25 us -> 15.2 us  [from_behind_2(): return lax.ppermute(array, axis, pairs)]
    dot_general x0 -> x6, matrix products: none -> 6.27 us  [the longest x3 2.81 us: rim_update(): jnp.einsum('snk,snr->srk', basis_rim, coefficients[None], precision=high)]
    ppermute x4 -> x2, waiting for transfers between devices: 8.69 us -> 2.96 us  [from_behind_2(): return lax.ppermute(array, axis, pairs)]
    slice x4 -> x11, local copies, waits for them, and re-layouts: 0.04 us -> 4.37 us  [the longest x1 1.01 us: shards(): next_device[starts[1]:starts[2]].reshape(1, nrhs, IFW)]
    ppermute x0 -> x1, starting transfers between devices: none -> 2.34 us  [shards(): incoming = lax.ppermute(outgoing, SPREAD, pairs)]
    select_n x0 -> x1, other arithmetic: none -> 1.39 us  [shards(): outgoing = jnp.where(is_last, to_last, to_first)]
    another operation x0 -> x2, local copies, waits for them, and re-layouts: none -> 1.32 us  [the longest x1 1.31 us: shards(): first_basis.reshape(-1)]
    all_gather x3, blocking collectives: 42.4 us -> 43.6 us  [shards(): gathered_in = lax.all_gather(gathered_in, axis, axis=0, tiled=True)]
  transfers between devices with their start and end apart: 4 -> 3, of which waited for: 2 -> 1; matrix products, arithmetic and copies ran while one was open for 0% -> 9% of each run, Pallas kernels for 0% -> 0%
where the time goes in v2:
time: 101 us; the launch traced here: 99.6 us
  blocking collectives  55.9 us (55%)
  starting transfers between devices  17.5 us (17%)
  matrix products  11.3 us (11%)
  local copies, waits for them, and re-layouts  8.68 us (9%)
  waiting for transfers between devices  2.96 us (3%)
  other arithmetic  2.92 us (3%)
    all_gather x3, blocking collectives, shards(): gathered_in = lax.all_gather(gathered_in, axis, axis=0, tiled=True)  43.6 us
    ppermute x2, starting transfers between devices, from_behind_2(): return lax.ppermute(array, axis, pairs)  15.2 us
    all_gather x1, blocking collectives, shards(): gathered = lax.all_gather(packed, 'sub', axis=0, tiled=False)  12.2 us
    ppermute x2, waiting for transfers between devices, from_behind_2(): return lax.ppermute(array, axis, pairs)  2.96 us
    dot_general x3, matrix products, rim_update(): jnp.einsum('snk,snr->srk', basis_rim, coefficients[None], precision=high)  2.81 us
    ppermute x1, starting transfers between devices, shards(): incoming = lax.ppermute(outgoing, SPREAD, pairs)  2.34 us
  transfers between devices with their start and end apart: 3, of which 1 were waited for; matrix products, arithmetic and copies ran while one was open for 9% of the time, Pallas kernels for 0%

profile of v2, /device:TPU:2, one launch (start us, length us, event | category | flops | bytes accessed | tf_op | source)
XLA Modules:
  0.0 99.6 jit_solution(17266841809985329876)
XLA Ops:
  0.0 1.1 %copy.28 = f32[4,32,512]{2,1,0:T(8,128)S(1)} copy(f32[4,32,512]{2,1,0:T(8,128)} %param.14) | data formatting | bytes 524288
  1.1 13.3 %collective-permute-start.1 = (f32[1,32,128]{2,1,0:T(8,128)S(1)}, f32[1,32,128]{2,1,0:T(8,128)S(1)}, u32[]{:S(2)}, u32[]{:S(2)}) collective-permute-start(f32[1,32,128]{2,1,0:T(8,128)S(1)} %get-tuple-element.59), channel_id=1, source_target_pairs={{1,0},{2,1},{3,2},{4,3},{5,4},{6,5},{7,6},{8,7},{9,8},{10,9},{11,1... | collective-permute-start | bytes 49160 | tf_op jit(solution)/shard_map/ppermute | solution.py:13
  14.4 1.9 %collective-permute-start = (f32[1,32,128]{2,1,0:T(8,128)S(1)}, f32[1,32,128]{2,1,0:T(8,128)S(1)}, u32[]{:S(2)}, u32[]{:S(2)}) collective-permute-start(f32[1,32,128]{2,1,0:T(8,128)S(1)} %get-tuple-element.60), channel_id=1, source_target_pairs={{0,1},{1,2},{2,3},{3,4},{4,5},{5,6},{6,7},{7,8},{8,9},{9,10},{10,1... | collective-permute-start | bytes 49160 | tf_op jit(solution)/shard_map/ppermute | solution.py:13
  16.3 1.3 %slice_bitcast_fusion.6 = (f32[1024]{0:T(1024)}, f32[1024]{0:T(1024)}) fusion(f32[4,8,512]{2,1,0:T(8,128)} %param.16), kind=kLoop, calls=%fused_computation.44 | loop fusion | bytes 16384 | tf_op jit(solution)/shard_map/reshape;squeeze | solution.py:58
  17.6 1.4 %convolution_bitcast_fusion = f32[1,32,8,128]{3,2,1,0:T(8,128)S(1)} fusion(f32[32,4096]{1,0:T(8,128)} %param.19, f32[32,128]{1,0:T(8,128)} %bitcast.82), kind=kOutput, calls=%fused_computation.1 | convolution fusion | flops 12582912 | bytes 671744 | tf_op jit(solution)/shard_map/dot_general | solution.py:66
  19.1 1.5 %convolution_bitcast_fusion.1 = f32[1,32,8,128]{3,2,1,0:T(8,128)S(1)} fusion(f32[32,4096]{1,0:T(8,128)} %param.19, f32[32,128]{1,0:T(8,128)} %bitcast.83), kind=kOutput, calls=%fused_computation.2 | convolution fusion | flops 12582912 | bytes 671744 | tf_op jit(solution)/shard_map/dot_general | solution.py:65
  20.7 3.0 %collective-permute-done = f32[1,32,128]{2,1,0:T(8,128)S(1)} collective-permute-done((f32[1,32,128]{2,1,0:T(8,128)S(1)}, f32[1,32,128]{2,1,0:T(8,128)S(1)}, u32[]{:S(2)}, u32[]{:S(2)}) %collective-permute-start) | collective-permute-done | bytes 16416 | tf_op jit(solution)/shard_map/ppermute | solution.py:13
  24.9 12.2 %all-gather = f32[45056]{0:T(1024)S(1)} all-gather(f32[11264]{0:T(1024)S(1)} %constant_dynamic-update-slice_fusion.1), channel_id=2, replica_groups=mesh['x'=4,'z'=16,'core'=2,'sub'=4] {'sub'}, dimensions={0}, use_global_device_ids=true | all-gather | bytes 225280 | tf_op jit(solution)/shard_map/all_gather | solution.py:59
  37.2 0.7 reshape.223
  39.0 1.1 %convolution_bitcast_fusion.4 = f32[128,32]{0,1:T(8,128)S(1)} fusion(f32[128,32]{1,0:T(8,128)S(1)} %reshape.211, f32[1,128,128]{2,1,0:T(8,128)} %param.17), kind=kOutput, calls=%fused_computation.12 | convolution fusion | flops 6291456 | bytes 98304 | tf_op jit(solution)/shard_map/dot_general | solution.py:61
  40.2 1.8 %all_gather.17 = f32[64,32]{1,0:T(8,128)S(1)} all-gather(f32[32,32]{1,0:T(8,128)S(1)} %copy.11), channel_id=1, replica_groups=mesh['x'=4,'z'=16,'core'=2,'sub'=4] {'core'}, dimensions={0}, use_global_device_ids=true | all-gather | bytes 12288 | tf_op jit(solution)/shard_map/all_gather | solution.py:78
  42.4 1.4 %maximum_select_fusion = f32[38144]{0:T(1024)} fusion(f32[256]{0:T(256)S(1)} %reshape.216, f32[32768]{0:T(1024)S(1)} %bitcast.81, f32[1024]{0:T(1024)} %get-tuple-element.66, f32[4096]{0:T(1024)S(1)} %get-tuple-element.56, f32[256]{0:T(256)S(1)} %reshape.218, f32[32768]{0:T(1024)S(1)} %bitcast.80, f32[1024]{0:T(1024)} %get-tuple-element.65, ...), kind=kLoop, calls=%fused_computation.14 | loop fusion | flops 267008 | bytes 457729 | tf_op jit(solution)/shard_map/jit(_where)/select_n | solution.py:71
  43.8 2.3 %collective-permute-start.2 = (f32[38144]{0:T(1024)}, f32[38144]{0:T(1024)}, u32[]{:S(2)}, u32[]{:S(2)}) collective-permute-start(f32[38144]{0:T(1024)} %maximum_select_fusion), channel_id=1, source_target_pairs={{3,4},{7,8},{11,12},{15,16},{19,20},{23,24},{27,28},{31,32},{35,36... | collective-permute-start | bytes 457736 | tf_op jit(solution)/shard_map/ppermute | solution.py:74
  46.1 28.7 %all-gather.1 = f32[16,64,32]{1,2,0:T(8,128)S(1)} all-gather(f32[1,64,32]{1,2,0:T(8,128)S(1)} %copy.12), channel_id=1, replica_groups=mesh['x'=4,'z'=16,'core'=2,'sub'=4] {'z'}, dimensions={0}, use_global_device_ids=true | all-gather | bytes 139264 | tf_op jit(solution)/shard_map/all_gather | solution.py:78
  75.1 13.1 %all_gather.19 = f32[4096,32]{0,1:T(8,128)S(1)} all-gather(f32[1024,32]{0,1:T(8,128)S(1)} %reshape.225), channel_id=1, replica_groups=mesh['x'=4,'z'=16,'core'=2,'sub'=4] {'x'}, dimensions={0}, use_global_device_ids=true | all-gather | bytes 655360 | tf_op jit(solution)/shard_map/all_gather | solution.py:78
  88.8 0.9 fusion.4
  89.8 1.3 %convolution_add_fusion = f32[4,32,512]{2,1,0:T(8,128)S(1)} fusion(f32[4,32,512]{2,1,0:T(8,128)S(1)} %fusion.5, f32[4,8,512]{2,1,0:T(8,128)} %param.16, f32[32,32]{1,0:T(8,128)S(1)} %copy.14), kind=kOutput, calls=%fused_computation | convolution fusion | flops 6356992 | bytes 593920 | tf_op jit(solution)/shard_map/snk,snr->srk/dot_general | solution.py:84
  91.1 1.0 %fusion.29 = (f32[1,4096]{1,0:T(1,128)S(1)}, f32[1,4096]{1,0:T(1,128)S(1)}) fusion(f32[4,11264]{1,0:T(4,128)} %reshape.223, s32[]{:T(128)S(6)} %select_n.50, s32[]{:T(128)S(6)} %add.88, s32[]{:T(128)S(6)} %max.3, s32[]{:T(128)S(6)} %add.86), kind=kLoop, calls=%fused_computation.58 | loop fusion | bytes 65552 | tf_op jit(solution)/shard_map/slice | solution.py:103
  92.1 0.8 fusion.28
  93.7 0.9 slice.247
  95.2 0.9 fusion.19
  96.1 0.9 fusion.3
  97.1 1.0 fusion.1
  98.1 1.5 %fusion.7 = f32[4,32,512]{2,1,0:T(8,128)} fusion(f32[4,32,512]{2,1,0:T(8,128)} %copy-done.2, f32[1,32,128]{2,1,0:T(8,128)S(1)} %fusion.1, f32[3,32,128]{2,1,0:T(8,128)S(1)} %get-tuple-element.53), kind=kLoop, calls=%fused_computation.18 | loop fusion | flops 49152 | bytes 196608 | tf_op jit(solution)/shard_map/scatter-add | solution.py:30
  (48 shorter events, 5.2 us)
Async XLA Ops:
  0.0 24.1 %copy-start = (bf16[4,512,512]{2,1,0:T(8,128)(2,1)S(1)}, bf16[4,512,512]{2,1,0:T(8,128)(2,1)}, u32[]{:S(2)}) copy-start(bf16[4,512,512]{2,1,0:T(8,128)(2,1)} %param.15) | copy-start | bytes 6291460
  0.0 23.7 %copy-start.3 = (f32[4,8,512]{2,1,0:T(8,128)S(1)}, f32[4,8,512]{2,1,0:T(8,128)}, u32[]{:S(2)}) copy-start(f32[4,8,512]{2,1,0:T(8,128)} %param.16) | copy-start | bytes 196612
  1.1 22.6 %collective-permute-start.1 = (f32[1,32,128]{2,1,0:T(8,128)S(1)}, f32[1,32,128]{2,1,0:T(8,128)S(1)}, u32[]{:S(2)}, u32[]{:S(2)}) collective-permute-start(f32[1,32,128]{2,1,0:T(8,128)S(1)} %get-tuple-element.59), channel_id=1, source_target_pairs={{1,0},{2,1},{3,2},{4,3},{5,4},{6,5},{7,6},{8,7},{9,8},{10,9},{11,1... | collective-permute-start | bytes 49160 | tf_op jit(solution)/shard_map/ppermute | solution.py:13
  14.4 9.3 %collective-permute-start = (f32[1,32,128]{2,1,0:T(8,128)S(1)}, f32[1,32,128]{2,1,0:T(8,128)S(1)}, u32[]{:S(2)}, u32[]{:S(2)}) collective-permute-start(f32[1,32,128]{2,1,0:T(8,128)S(1)} %get-tuple-element.60), channel_id=1, source_target_pairs={{0,1},{1,2},{2,3},{3,4},{4,5},{5,6},{6,7},{7,8},{8,9},{9,10},{10,1... | collective-permute-start | bytes 49160 | tf_op jit(solution)/shard_map/ppermute | solution.py:13
  23.7 15.1 %copy-start.4 = (f32[1,32,128]{2,1,0:T(8,128)S(1)}, f32[1,32,128]{2,1,0:T(8,128)}, u32[]{:S(2)}) copy-start(f32[1,32,128]{2,1,0:T(8,128)} %param.18) | copy-start | bytes 49156
  24.9 63.4 %copy-start.1 = (f32[32,4096]{1,0:T(8,128)S(1)}, f32[32,4096]{1,0:T(8,128)}, u32[]{:S(2)}) copy-start(f32[32,4096]{1,0:T(8,128)} %param.19) | copy-start | bytes 1572868
  43.8 49.2 %collective-permute-start.2 = (f32[38144]{0:T(1024)}, f32[38144]{0:T(1024)}, u32[]{:S(2)}, u32[]{:S(2)}) collective-permute-start(f32[38144]{0:T(1024)} %maximum_select_fusion), channel_id=1, source_target_pairs={{3,4},{7,8},{11,12},{15,16},{19,20},{23,24},{27,28},{31,32},{35,36... | collective-permute-start | bytes 457736 | tf_op jit(solution)/shard_map/ppermute | solution.py:74
  97.1 1.0 %copy-start.2 = (f32[4,32,512]{2,1,0:T(8,128)}, f32[4,32,512]{2,1,0:T(8,128)S(1)}, u32[]{:S(2)}) copy-start(f32[4,32,512]{2,1,0:T(8,128)S(1)} %fusion.8) | copy-start | bytes 786436

commit v3 on v2

--- a/solution.py
+++ b/solution.py
@@ -51,24 +51,27 @@
     last_local = local[-1, :, nloc - IFW :]
     first_basis = coarse_basis[0, :, :IFW]
     last_basis = coarse_basis[-1, :, nloc - IFW :]
-    sizes = [coarse.size, nrhs * IFW, nrhs * IFW, nc * IFW, nc * IFW]
-    starts = [sum(sizes[:i]) for i in range(len(sizes) + 1)]
+    coarse_rows = coarse.size // IFW
+    rows = [coarse_rows, nrhs, nrhs, nc, nc]
+    at = [sum(rows[:i]) for i in range(len(rows) + 1)]
     packed = jnp.concatenate(
-        [coarse.reshape(-1), first_local.reshape(-1), last_local.reshape(-1),
-         first_basis.reshape(-1), last_basis.reshape(-1)], 0)
+        [coarse.reshape(coarse_rows, IFW), first_local, last_local, first_basis, last_basis], 0)
     gathered = lax.all_gather(packed, "sub", axis=0, tiled=False)
-    groups = gathered[:, : starts[1]].reshape(-1, nrhs)
+    groups = gathered[:, : at[1]].reshape(-1, nrhs)
     level2 = jnp.dot(level2_inverse[0], groups, precision=high)
     level3_in = jnp.dot(level2_basis[0], groups, precision=high)
 
     is_last = position == sub - 1
-    last_fold = jnp.dot(level2_basis[0][:, -nc:].T, level3_inverse, precision=high)
-    first_fold = jnp.dot(level2_basis[0][:, :nc].T, level3_inverse, precision=high)
-    to_last = jnp.concatenate(
-        [last_local.reshape(-1), last_basis.reshape(-1), last_fold.reshape(-1), level2[-nc:].reshape(-1)], 0)
-    to_first = jnp.concatenate(
-        [first_local.reshape(-1), first_basis.reshape(-1), first_fold.reshape(-1), level2[:nc].reshape(-1)], 0)
-    outgoing = jnp.where(is_last, to_last, to_first)
+    n3 = level3_inverse.shape[1]
+    pick = jnp.where(is_last, level2_basis[0][:, -nc:], level2_basis[0][:, :nc])
+    fold = jnp.dot(pick.T, level3_inverse, precision=high)
+    edge_rows = jnp.where(is_last, level2[-nc:], level2[:nc])
+    edge_local = jnp.where(is_last, last_local, first_local)
+    edge_basis = jnp.where(is_last, last_basis, first_basis)
+    cut = [nrhs, nc, nc * n3 // IFW, nc * nrhs // IFW]
+    on = [sum(cut[:i]) for i in range(len(cut) + 1)]
+    outgoing = jnp.concatenate(
+        [edge_local, edge_basis, fold.reshape(-1, IFW), edge_rows.reshape(-1, IFW)], 0)
     count = lax.axis_size(SPREAD)
     pairs = [(i, i + 1) for i in range(sub - 1, count - 1, sub)] + [(i + 1, i) for i in range(sub - 1, count - 1, sub)]
     incoming = lax.ppermute(outgoing, SPREAD, pairs)
@@ -83,27 +86,23 @@
     per_sub = own_rows.reshape(coarse.shape[0], coarse.shape[1], -1)
     update = local + jnp.einsum("snk,snr->srk", coarse_basis, per_sub, precision=high)
 
-    cut = [nrhs * IFW, nc * IFW, nc * level3_inverse.shape[1], nc * nrhs]
-    at = [sum(cut[:i]) for i in range(len(cut) + 1)]
-    cross_local = incoming[at[0] : at[1]].reshape(1, nrhs, IFW)
-    cross_basis = incoming[at[1] : at[2]].reshape(1, nc, IFW)
-    cross_fold = incoming[at[2] : at[3]].reshape(nc, -1)
-    cross_rows = incoming[at[3] : at[4]].reshape(nc, nrhs)
+    cross_fold = incoming[on[2] : on[3]].reshape(nc, n3)
+    cross_rows = incoming[on[3] : on[4]].reshape(nc, nrhs)
     cross_coef = cross_rows + jnp.dot(cross_fold, gathered_in, precision=high)
-    cross_rim = rim_update(cross_local, cross_basis, cross_coef)
 
     prev_device = lax.dynamic_index_in_dim(gathered, jnp.maximum(position - 1, 0), 0, keepdims=False)
     next_device = lax.dynamic_index_in_dim(gathered, jnp.minimum(position + 1, sub - 1), 0, keepdims=False)
     prev_rows = lax.dynamic_slice_in_dim(corrected, position * own_count - nc, nc, 0)
     next_rows = lax.dynamic_slice_in_dim(corrected, (position + 1) * own_count, nc, 0)
-    inner_before = rim_update(
-        prev_device[starts[2] : starts[3]].reshape(1, nrhs, IFW),
-        prev_device[starts[4] : starts[5]].reshape(1, nc, IFW), prev_rows)
-    inner_behind = rim_update(
-        next_device[starts[1] : starts[2]].reshape(1, nrhs, IFW),
-        next_device[starts[3] : starts[4]].reshape(1, nc, IFW), next_rows)
-    from_before = jnp.where(position > 0, inner_before, cross_rim)
-    from_behind = jnp.where(is_last, cross_rim, inner_behind)
+    first = position == 0
+    before_local = jnp.where(first, incoming[on[0] : on[1]], prev_device[at[2] : at[3]])
+    before_basis = jnp.where(first, incoming[on[1] : on[2]], prev_device[at[4] : at[5]])
+    before_coef = jnp.where(first, cross_coef, prev_rows)
+    behind_local = jnp.where(is_last, incoming[on[0] : on[1]], next_device[at[1] : at[2]])
+    behind_basis = jnp.where(is_last, incoming[on[1] : on[2]], next_device[at[3] : at[4]])
+    behind_coef = jnp.where(is_last, cross_coef, next_rows)
+    from_before = rim_update(before_local[None], before_basis[None], before_coef)
+    from_behind = rim_update(behind_local[None], behind_basis[None], behind_coef)
     return add_rims(update, from_before, from_behind)
 
 

time: 101 us -> 91.9 us (0.910)
  the two profiles are of different devices: /device:TPU:2 before, /device:TPU:24 now
where the time goes in v3:
time: 91.9 us; the launch traced here: 91.3 us
  blocking collectives  67.4 us (73%)
  matrix products  8.31 us (9%)
  starting transfers between devices  7.74 us (8%)
  local copies, waits for them, and re-layouts  4.59 us (5%)
  other arithmetic  2.35 us (3%)
    all_gather x3, blocking collectives, shards(): gathered_in = lax.all_gather(gathered_in, axis, axis=0, tiled=True)  53.4 us
    all_gather x1, blocking collectives, shards(): gathered = lax.all_gather(packed, 'sub', axis=0, tiled=False)  14 us
    ppermute x2, starting transfers between devices, from_behind_2(): return lax.ppermute(array, axis, pairs)  5.83 us
    dot_general x2, matrix products, rim_update(): jnp.einsum('snk,snr->srk', basis_rim, coefficients[None], precision=high)  2.01 us
    ppermute x1, starting transfers between devices, shards(): incoming = lax.ppermute(outgoing, SPREAD, pairs)  1.91 us
  transfers between devices with their start and end apart: 3, of which 1 were waited for; matrix products, arithmetic and copies ran while one was open for 5% of the time, Pallas kernels for 0%

profile of v3, /device:TPU:24, one launch (start us, length us, event | category | flops | bytes accessed | tf_op | source)
XLA Modules:
  0.0 91.3 jit_solution(8529809995937637141)
XLA Ops:
  0.0 1.1 %copy.32 = f32[4,32,512]{2,1,0:T(8,128)S(1)} copy(f32[4,32,512]{2,1,0:T(8,128)} %param.14) | data formatting | bytes 524288
  1.1 1.9 %collective-permute-start = (f32[1,32,128]{2,1,0:T(8,128)S(1)}, f32[1,32,128]{2,1,0:T(8,128)S(1)}, u32[]{:S(2)}, u32[]{:S(2)}) collective-permute-start(f32[1,32,128]{2,1,0:T(8,128)S(1)} %get-tuple-element.60), channel_id=1, source_target_pairs={{0,1},{1,2},{2,3},{3,4},{4,5},{5,6},{6,7},{7,8},{8,9},{9,10},{10,1... | collective-permute-start | bytes 49160 | tf_op jit(solution)/shard_map/ppermute | solution.py:13
  3.0 3.9 %collective-permute-start.1 = (f32[1,32,128]{2,1,0:T(8,128)S(1)}, f32[1,32,128]{2,1,0:T(8,128)S(1)}, u32[]{:S(2)}, u32[]{:S(2)}) collective-permute-start(f32[1,32,128]{2,1,0:T(8,128)S(1)} %get-tuple-element.59), channel_id=1, source_target_pairs={{1,0},{2,1},{3,2},{4,3},{5,4},{6,5},{7,6},{8,7},{9,8},{10,9},{11,1... | collective-permute-start | bytes 49160 | tf_op jit(solution)/shard_map/ppermute | solution.py:13
  7.0 1.6 %fusion.15 = f32[8,4096]{1,0:T(8,128)S(1)} fusion(f32[32,4096]{1,0:T(8,128)} %param.19, f32[32,128]{1,0:T(8,128)} %bitcast.85, pred[]{:T(512)S(6)} %eq.7), kind=kOutput, calls=%fused_computation.32 | convolution fusion | flops 12583168 | bytes 688129 | tf_op jit(solution)/shard_map/dot_general | solution.py:67
  8.7 0.6 collective-permute-done.1
  9.3 0.7 fusion.1
  10.1 0.3 convolution_bitcast_fusion.3
  10.5 14.0 %all-gather = f32[352,128]{1,0:T(8,128)} all-gather(f32[88,128]{1,0:T(8,128)S(1)} %constant_dynamic-update-slice_fusion), channel_id=2, replica_groups=mesh['x'=4,'z'=16,'core'=2,'sub'=4] {'sub'}, dimensions={0}, use_global_device_ids=true | all-gather | bytes 225280 | tf_op jit(solution)/shard_map/all_gather | solution.py:59
  24.5 0.7 slice.225
  25.3 0.2 convolution_bitcast_fusion.1
  26.0 0.7 pad_maximum_fusion
  26.7 1.9 %collective-permute-start.2 = (f32[298,128]{1,0:T(8,128)}, f32[298,128]{1,0:T(8,128)}, u32[]{:S(2)}, u32[]{:S(2)}) collective-permute-start(f32[298,128]{1,0:T(8,128)} %pad_maximum_fusion), channel_id=1, source_target_pairs={{3,4},{7,8},{11,12},{15,16},{19,20},{23,24},{27,28},{31,32},{35,36... | collective-permute-start | bytes 457736 | tf_op jit(solution)/shard_map/ppermute | solution.py:77
  28.7 3.3 %all_gather.17 = f32[64,32]{1,0:T(8,128)S(1)} all-gather(f32[32,32]{1,0:T(8,128)S(1)} %copy.15), channel_id=1, replica_groups=mesh['x'=4,'z'=16,'core'=2,'sub'=4] {'core'}, dimensions={0}, use_global_device_ids=true | all-gather | bytes 12288 | tf_op jit(solution)/shard_map/all_gather | solution.py:81
  32.0 37.1 %all-gather.1 = f32[16,64,32]{1,2,0:T(8,128)S(1)} all-gather(f32[1,64,32]{1,2,0:T(8,128)S(1)} %copy.16), channel_id=1, replica_groups=mesh['x'=4,'z'=16,'core'=2,'sub'=4] {'z'}, dimensions={0}, use_global_device_ids=true | all-gather | bytes 139264 | tf_op jit(solution)/shard_map/all_gather | solution.py:81
  69.4 13.1 %all_gather.19 = f32[4096,32]{0,1:T(8,128)S(1)} all-gather(f32[1024,32]{0,1:T(8,128)S(1)} %reshape.162), channel_id=1, replica_groups=mesh['x'=4,'z'=16,'core'=2,'sub'=4] {'x'}, dimensions={0}, use_global_device_ids=true | all-gather | bytes 655360 | tf_op jit(solution)/shard_map/all_gather | solution.py:81
  82.5 0.5 fusion.51
  83.1 0.9 fusion
  84.1 1.3 %convolution_add_fusion = f32[4,32,512]{2,1,0:T(8,128)S(1)} fusion(f32[4,32,512]{2,1,0:T(8,128)S(1)} %fusion.1, f32[4,8,512]{2,1,0:T(8,128)} %param.16, f32[32,32]{1,0:T(8,128)S(1)} %copy.18), kind=kOutput, calls=%fused_computation | convolution fusion | flops 6356992 | bytes 593920 | tf_op jit(solution)/shard_map/snk,snr->srk/dot_general | solution.py:87
  85.4 0.9 %slice.233 = f32[256,128]{1,0:T(8,128)S(1)} slice(f32[298,128]{1,0:T(8,128)} %collective-permute-done.2), slice={[40:296], [0:128]} | slice | bytes 262144 | tf_op jit(solution)/shard_map/slice | solution.py:89
  86.4 0.5 fusion.52
  86.9 0.7 slice.232
  87.8 1.0 %fusion.14 = f32[1,32,128]{2,1,0:T(8,128)S(1)} fusion(f32[4,88,128]{2,1,0:T(8,128)} %bitcast.5, s32[]{:T(128)S(6)} %max.3, s32[]{:T(128)S(6)} %add.87, f32[128,32]{0,1:T(8,128)S(1)} %fusion, s32[]{:T(128)S(6)} %select_n.88, f32[298,128]{1,0:T(8,128)} %collective-permute-done.2, pred[]{:T(512)S(6)} %eq.6, f32[8,32]{0,1:T(8,128)S(1)} %copy.20, ...), kind=kOutput, calls=%fused_computation.29 | convolution fusion | flops 402944 | bytes 79872 | tf_op jit(solution)/shard_map/snk,snr->srk/dot_general | solution.py:35
  88.7 1.1 %fusion.11 = f32[1,32,128]{2,1,0:T(8,128)S(1)} fusion(f32[4,88,128]{2,1,0:T(8,128)} %bitcast.5, s32[]{:T(128)S(6)} %select_n.92, s32[]{:T(128)S(6)} %add.89, f32[128,32]{0,1:T(8,128)S(1)} %fusion, s32[]{:T(128)S(6)} %select_n.94, f32[298,128]{1,0:T(8,128)} %collective-permute-done.2, pred[]{:T(512)S(6)} %eq.7, f32[8,32]{0,1:T(8,128)S(1)} %copy.20, ...), kind=kOutput, calls=%fused_computation.25 | convolution fusion | flops 402944 | bytes 79872 | tf_op jit(solution)/shard_map/snk,snr->srk/dot_general | solution.py:35
  89.8 1.5 %fusion.3 = f32[4,32,512]{2,1,0:T(8,128)} fusion(f32[4,32,512]{2,1,0:T(8,128)} %copy-done.2, f32[1,32,128]{2,1,0:T(8,128)S(1)} %fusion.11, f32[3,32,128]{2,1,0:T(8,128)S(1)} %get-tuple-element.53), kind=kLoop, calls=%fused_computation.10 | loop fusion | flops 49152 | bytes 196608 | tf_op jit(solution)/shard_map/scatter-add | solution.py:30
  (41 shorter events, 1.6 us)
Async XLA Ops:
  0.0 9.3 %copy-start = (bf16[4,512,512]{2,1,0:T(8,128)(2,1)S(1)}, bf16[4,512,512]{2,1,0:T(8,128)(2,1)}, u32[]{:S(2)}) copy-start(bf16[4,512,512]{2,1,0:T(8,128)(2,1)} %param.15) | copy-start | bytes 6291460
  1.1 7.5 %collective-permute-start = (f32[1,32,128]{2,1,0:T(8,128)S(1)}, f32[1,32,128]{2,1,0:T(8,128)S(1)}, u32[]{:S(2)}, u32[]{:S(2)}) collective-permute-start(f32[1,32,128]{2,1,0:T(8,128)S(1)} %get-tuple-element.60), channel_id=1, source_target_pairs={{0,1},{1,2},{2,3},{3,4},{4,5},{5,6},{6,7},{7,8},{8,9},{9,10},{10,1... | collective-permute-start | bytes 49160 | tf_op jit(solution)/shard_map/ppermute | solution.py:13
  3.0 6.3 %collective-permute-start.1 = (f32[1,32,128]{2,1,0:T(8,128)S(1)}, f32[1,32,128]{2,1,0:T(8,128)S(1)}, u32[]{:S(2)}, u32[]{:S(2)}) collective-permute-start(f32[1,32,128]{2,1,0:T(8,128)S(1)} %get-tuple-element.59), channel_id=1, source_target_pairs={{1,0},{2,1},{3,2},{4,3},{5,4},{6,5},{7,6},{8,7},{9,8},{10,9},{11,1... | collective-permute-start | bytes 49160 | tf_op jit(solution)/shard_map/ppermute | solution.py:13
  7.0 3.1 %copy-start.3 = (f32[4,8,512]{2,1,0:T(8,128)S(1)}, f32[4,8,512]{2,1,0:T(8,128)}, u32[]{:S(2)}) copy-start(f32[4,8,512]{2,1,0:T(8,128)} %param.16) | copy-start | bytes 196612
  8.6 16.7 %copy-start.4 = (f32[1,32,128]{2,1,0:T(8,128)S(1)}, f32[1,32,128]{2,1,0:T(8,128)}, u32[]{:S(2)}) copy-start(f32[1,32,128]{2,1,0:T(8,128)} %param.18) | copy-start | bytes 49156
  8.6 16.9 %copy-start.5 = (f32[1,128,128]{2,1,0:T(8,128)S(1)}, f32[1,128,128]{2,1,0:T(8,128)}, u32[]{:S(2)}) copy-start(f32[1,128,128]{2,1,0:T(8,128)} %param.17) | copy-start | bytes 196612
  10.0 72.5 %copy-start.1 = (f32[32,4096]{1,0:T(8,128)S(1)}, f32[32,4096]{1,0:T(8,128)}, u32[]{:S(2)}) copy-start(f32[32,4096]{1,0:T(8,128)} %param.19) | copy-start | bytes 1572868
  26.7 58.7 %collective-permute-start.2 = (f32[298,128]{1,0:T(8,128)}, f32[298,128]{1,0:T(8,128)}, u32[]{:S(2)}, u32[]{:S(2)}) collective-permute-start(f32[298,128]{1,0:T(8,128)} %pad_maximum_fusion), channel_id=1, source_target_pairs={{3,4},{7,8},{11,12},{15,16},{19,20},{23,24},{27,28},{31,32},{35,36... | collective-permute-start | bytes 457736 | tf_op jit(solution)/shard_map/ppermute | solution.py:77
  88.7 1.1 %copy-start.2 = (f32[4,32,512]{2,1,0:T(8,128)}, f32[4,32,512]{2,1,0:T(8,128)S(1)}, u32[]{:S(2)}) copy-start(f32[4,32,512]{2,1,0:T(8,128)S(1)} %fusion.4) | copy-start | bytes 786436

commit v4 on v3

--- a/solution.py
+++ b/solution.py
@@ -68,10 +68,11 @@
     edge_rows = jnp.where(is_last, level2[-nc:], level2[:nc])
     edge_local = jnp.where(is_last, last_local, first_local)
     edge_basis = jnp.where(is_last, last_basis, first_basis)
-    cut = [nrhs, nc, nc * n3 // IFW, nc * nrhs // IFW]
+    fold_rows = nc * n3 // IFW
+    cut = [fold_rows, nrhs, nc, nc]
     on = [sum(cut[:i]) for i in range(len(cut) + 1)]
     outgoing = jnp.concatenate(
-        [edge_local, edge_basis, fold.reshape(-1, IFW), edge_rows.reshape(-1, IFW)], 0)
+        [fold.reshape(fold_rows, IFW), edge_local, edge_basis, jnp.pad(edge_rows, ((0, 0), (0, IFW - nrhs)))], 0)
     count = lax.axis_size(SPREAD)
     pairs = [(i, i + 1) for i in range(sub - 1, count - 1, sub)] + [(i + 1, i) for i in range(sub - 1, count - 1, sub)]
     incoming = lax.ppermute(outgoing, SPREAD, pairs)
@@ -86,8 +87,8 @@
     per_sub = own_rows.reshape(coarse.shape[0], coarse.shape[1], -1)
     update = local + jnp.einsum("snk,snr->srk", coarse_basis, per_sub, precision=high)
 
-    cross_fold = incoming[on[2] : on[3]].reshape(nc, n3)
-    cross_rows = incoming[on[3] : on[4]].reshape(nc, nrhs)
+    cross_fold = incoming[: on[1]].reshape(nc, n3)
+    cross_rows = incoming[on[3] : on[4], :nrhs]
     cross_coef = cross_rows + jnp.dot(cross_fold, gathered_in, precision=high)
 
     prev_device = lax.dynamic_index_in_dim(gathered, jnp.maximum(position - 1, 0), 0, keepdims=False)
@@ -95,14 +96,20 @@
     prev_rows = lax.dynamic_slice_in_dim(corrected, position * own_count - nc, nc, 0)
     next_rows = lax.dynamic_slice_in_dim(corrected, (position + 1) * own_count, nc, 0)
     first = position == 0
-    before_local = jnp.where(first, incoming[on[0] : on[1]], prev_device[at[2] : at[3]])
-    before_basis = jnp.where(first, incoming[on[1] : on[2]], prev_device[at[4] : at[5]])
-    before_coef = jnp.where(first, cross_coef, prev_rows)
-    behind_local = jnp.where(is_last, incoming[on[0] : on[1]], next_device[at[1] : at[2]])
-    behind_basis = jnp.where(is_last, incoming[on[1] : on[2]], next_device[at[3] : at[4]])
-    behind_coef = jnp.where(is_last, cross_coef, next_rows)
-    from_before = rim_update(before_local[None], before_basis[None], before_coef)
-    from_behind = rim_update(behind_local[None], behind_basis[None], behind_coef)
+    cross_local = incoming[on[1] : on[2]]
+    cross_basis = incoming[on[2] : on[3]]
+    rim_local = jnp.stack([
+        jnp.where(first, cross_local, prev_device[at[2] : at[3]]),
+        jnp.where(is_last, cross_local, next_device[at[1] : at[2]])])
+    rim_basis = jnp.stack([
+        jnp.where(first, cross_basis, prev_device[at[4] : at[5]]),
+        jnp.where(is_last, cross_basis, next_device[at[3] : at[4]])])
+    rim_coef = jnp.stack([
+        jnp.where(first, cross_coef, prev_rows),
+        jnp.where(is_last, cross_coef, next_rows)])
+    rims = rim_local + jnp.sum(rim_basis[:, :, None, :] * rim_coef[:, :, :, None], axis=1)
+    from_before = rims[0:1]
+    from_behind = rims[1:2]
     return add_rims(update, from_before, from_behind)
 
 

time: 91.9 us -> 91.9 us (level)
  other arithmetic: 2.35 us -> 3.85 us
  matrix products: 8.31 us -> 7.22 us
    dot_general x2 -> x0, matrix products: 2.01 us -> none  [rim_update(): jnp.einsum('snk,snr->srk', basis_rim, coefficients[None], precision=high)]
    another operation x0 -> x4, other arithmetic: none -> 1.48 us  [the longest x1 0.77 us: shards(): jnp.stack([jnp.where(first, cross_local, prev_device[at[2]:at[3]]), jnp.w...]
    unnamed x17 -> x19, local copies, waits for them, and re-layouts: 1.37 us -> 2.06 us
where the time goes in v4:
time: 91.9 us; the launch traced here: 91.3 us
  blocking collectives  67.4 us (73%)
  starting transfers between devices  7.74 us (8%)
  matrix products  7.22 us (8%)
  local copies, waits for them, and re-layouts  4.16 us (5%)
  other arithmetic  3.85 us (4%)
    all_gather x3, blocking collectives, shards(): gathered_in = lax.all_gather(gathered_in, axis, axis=0, tiled=True)  53.4 us
    all_gather x1, blocking collectives, shards(): gathered = lax.all_gather(packed, 'sub', axis=0, tiled=False)  14 us
    ppermute x2, starting transfers between devices, from_behind_2(): return lax.ppermute(array, axis, pairs)  5.83 us
    unnamed x19, local copies, waits for them, and re-layouts  2.06 us
    ppermute x1, starting transfers between devices, shards(): incoming = lax.ppermute(outgoing, SPREAD, pairs)  1.91 us
  transfers between devices with their start and end apart: 3, of which 1 were waited for; matrix products, arithmetic and copies ran while one was open for 5% of the time, Pallas kernels for 0%

profile of v4, /device:TPU:24, one launch (start us, length us, event | category | flops | bytes accessed | tf_op | source)
XLA Modules:
  0.0 91.3 jit_solution(3237160082649325740)
XLA Ops:
  0.0 1.1 %copy.33 = f32[4,32,512]{2,1,0:T(8,128)S(1)} copy(f32[4,32,512]{2,1,0:T(8,128)} %param.14) | data formatting | bytes 524288
  1.1 1.9 %collective-permute-start = (f32[1,32,128]{2,1,0:T(8,128)S(1)}, f32[1,32,128]{2,1,0:T(8,128)S(1)}, u32[]{:S(2)}, u32[]{:S(2)}) collective-permute-start(f32[1,32,128]{2,1,0:T(8,128)S(1)} %get-tuple-element.64), channel_id=1, source_target_pairs={{0,1},{1,2},{2,3},{3,4},{4,5},{5,6},{6,7},{7,8},{8,9},{9,10},{10,1... | collective-permute-start | bytes 49160 | tf_op jit(solution)/shard_map/ppermute | solution.py:13
  3.0 3.9 %collective-permute-start.1 = (f32[1,32,128]{2,1,0:T(8,128)S(1)}, f32[1,32,128]{2,1,0:T(8,128)S(1)}, u32[]{:S(2)}, u32[]{:S(2)}) collective-permute-start(f32[1,32,128]{2,1,0:T(8,128)S(1)} %get-tuple-element.63), channel_id=1, source_target_pairs={{1,0},{2,1},{3,2},{4,3},{5,4},{6,5},{7,6},{8,7},{9,8},{10,9},{11,1... | collective-permute-start | bytes 49160 | tf_op jit(solution)/shard_map/ppermute | solution.py:13
  7.0 1.6 %fusion.13 = f32[8,4096]{1,0:T(8,128)S(1)} fusion(f32[32,4096]{1,0:T(8,128)} %param.19, f32[32,128]{1,0:T(8,128)} %bitcast.91, pred[]{:T(512)S(6)} %eq.7), kind=kOutput, calls=%fused_computation.32 | convolution fusion | flops 12583168 | bytes 688129 | tf_op jit(solution)/shard_map/dot_general | solution.py:67
  8.7 0.6 collective-permute-done.1
  9.3 0.7 fusion.1
  10.1 0.3 convolution_bitcast_fusion.3
  10.5 14.0 %all-gather = f32[352,128]{1,0:T(8,128)} all-gather(f32[88,128]{1,0:T(8,128)S(1)} %constant_dynamic-update-slice_fusion), channel_id=2, replica_groups=mesh['x'=4,'z'=16,'core'=2,'sub'=4] {'sub'}, dimensions={0}, use_global_device_ids=true | all-gather | bytes 225280 | tf_op jit(solution)/shard_map/all_gather | solution.py:59
  24.5 0.7 slice.231
  25.3 0.2 convolution_bitcast_fusion.2
  25.8 0.7 select_maximum_fusion
  26.5 1.9 %collective-permute-start.2 = (f32[304,128]{1,0:T(8,128)}, f32[304,128]{1,0:T(8,128)}, u32[]{:S(2)}, u32[]{:S(2)}) collective-permute-start(f32[304,128]{1,0:T(8,128)} %select_maximum_fusion), channel_id=1, source_target_pairs={{3,4},{7,8},{11,12},{15,16},{19,20},{23,24},{27,28},{31,32},{35,36... | collective-permute-start | bytes 466952 | tf_op jit(solution)/shard_map/ppermute | solution.py:78
  28.5 3.3 %all_gather.17 = f32[64,32]{1,0:T(8,128)S(1)} all-gather(f32[32,32]{1,0:T(8,128)S(1)} %copy.18), channel_id=1, replica_groups=mesh['x'=4,'z'=16,'core'=2,'sub'=4] {'core'}, dimensions={0}, use_global_device_ids=true | all-gather | bytes 12288 | tf_op jit(solution)/shard_map/all_gather | solution.py:82
  31.8 37.1 %all-gather.1 = f32[16,64,32]{1,2,0:T(8,128)S(1)} all-gather(f32[1,64,32]{1,2,0:T(8,128)S(1)} %copy.19), channel_id=1, replica_groups=mesh['x'=4,'z'=16,'core'=2,'sub'=4] {'z'}, dimensions={0}, use_global_device_ids=true | all-gather | bytes 139264 | tf_op jit(solution)/shard_map/all_gather | solution.py:82
  69.1 13.1 %all_gather.19 = f32[4096,32]{0,1:T(8,128)S(1)} all-gather(f32[1024,32]{0,1:T(8,128)S(1)} %reshape.144), channel_id=1, replica_groups=mesh['x'=4,'z'=16,'core'=2,'sub'=4] {'x'}, dimensions={0}, use_global_device_ids=true | all-gather | bytes 655360 | tf_op jit(solution)/shard_map/all_gather | solution.py:82
  82.3 0.5 fusion.32
  82.8 1.1 %fusion = f32[128,32]{1,0:T(8,128)S(1)} fusion(f32[128,32]{1,0:T(8,128)} %copy-done.4, f32[32,32]{1,0:T(8,128)S(1)} %fusion.32, f32[1,32,128]{2,1,0:T(8,128)S(1)} %copy-done.5), kind=kOutput, calls=%fused_computation.2 | convolution fusion | flops 1576960 | bytes 53248 | tf_op jit(solution)/shard_map/dot_general | solution.py:84
  84.0 1.3 %convolution_add_fusion = f32[4,32,512]{2,1,0:T(8,128)S(1)} fusion(f32[4,32,512]{2,1,0:T(8,128)S(1)} %fusion.1, f32[4,8,512]{2,1,0:T(8,128)} %param.16, f32[128,32]{1,0:T(8,128)S(1)} %fusion, s32[]{:T(128)S(6)} %select_n.76), kind=kOutput, calls=%fused_computation | convolution fusion | flops 6356992 | bytes 606212 | tf_op jit(solution)/shard_map/snk,snr->srk/dot_general | solution.py:88
  85.3 0.9 %slice.240 = f32[256,128]{1,0:T(8,128)S(1)} slice(f32[304,128]{1,0:T(8,128)} %collective-permute-done.2), slice={[0:256], [0:128]} | slice | bytes 262144 | tf_op jit(solution)/shard_map/slice | solution.py:90
  86.2 0.7 fusion.24
  86.9 1.2 %select_bitcast_fusion.1 = (f32[1,8,32]{2,1,0:T(8,128)S(1)}, f32[1,8,32]{2,1,0:T(8,128)S(1)}) fusion(f32[128,32]{1,0:T(8,128)S(1)} %fusion, s32[]{:T(128)S(6)} %select_n.93, pred[]{:T(512)S(6)} %eq.6, f32[304,128]{1,0:T(8,128)} %collective-permute-done.2, s32[]{:T(128)S(6)} %select_n.95, pred[]{:T(512)S(6)} %eq.7, f32[8,4096]{1,0:T(8,128)S(1)} %reshape.141, ...), kind=kOutput, calls=%fused_computation.57 | convolution fusion | flops 12583680 | bytes 660490 | tf_op jit(solution)/shard_map/dot_general | solution.py:92
  88.3 0.8 fusion.12
  89.1 0.7 copy-done.2
  89.8 1.5 %fusion.3 = f32[4,32,512]{2,1,0:T(8,128)} fusion(f32[4,32,512]{2,1,0:T(8,128)} %copy-done.2, f32[1,32,128]{2,1,0:T(8,128)S(1)} %get-tuple-element.69, f32[3,32,128]{2,1,0:T(8,128)S(1)} %get-tuple-element.57), kind=kLoop, calls=%fused_computation.12 | loop fusion | flops 49152 | bytes 196608 | tf_op jit(solution)/shard_map/scatter-add | solution.py:30
  (41 shorter events, 1.2 us)
Async XLA Ops:
  0.0 9.3 %copy-start = (bf16[4,512,512]{2,1,0:T(8,128)(2,1)S(1)}, bf16[4,512,512]{2,1,0:T(8,128)(2,1)}, u32[]{:S(2)}) copy-start(bf16[4,512,512]{2,1,0:T(8,128)(2,1)} %param.15) | copy-start | bytes 6291460
  1.1 7.5 %collective-permute-start = (f32[1,32,128]{2,1,0:T(8,128)S(1)}, f32[1,32,128]{2,1,0:T(8,128)S(1)}, u32[]{:S(2)}, u32[]{:S(2)}) collective-permute-start(f32[1,32,128]{2,1,0:T(8,128)S(1)} %get-tuple-element.64), channel_id=1, source_target_pairs={{0,1},{1,2},{2,3},{3,4},{4,5},{5,6},{6,7},{7,8},{8,9},{9,10},{10,1... | collective-permute-start | bytes 49160 | tf_op jit(solution)/shard_map/ppermute | solution.py:13
  3.0 6.3 %collective-permute-start.1 = (f32[1,32,128]{2,1,0:T(8,128)S(1)}, f32[1,32,128]{2,1,0:T(8,128)S(1)}, u32[]{:S(2)}, u32[]{:S(2)}) collective-permute-start(f32[1,32,128]{2,1,0:T(8,128)S(1)} %get-tuple-element.63), channel_id=1, source_target_pairs={{1,0},{2,1},{3,2},{4,3},{5,4},{6,5},{7,6},{8,7},{9,8},{10,9},{11,1... | collective-permute-start | bytes 49160 | tf_op jit(solution)/shard_map/ppermute | solution.py:13
  7.0 3.1 %copy-start.3 = (f32[4,8,512]{2,1,0:T(8,128)S(1)}, f32[4,8,512]{2,1,0:T(8,128)}, u32[]{:S(2)}) copy-start(f32[4,8,512]{2,1,0:T(8,128)} %param.16) | copy-start | bytes 196612
  8.6 16.7 %copy-start.5 = (f32[1,32,128]{2,1,0:T(8,128)S(1)}, f32[1,32,128]{2,1,0:T(8,128)}, u32[]{:S(2)}) copy-start(f32[1,32,128]{2,1,0:T(8,128)} %param.18) | copy-start | bytes 49156
  8.6 17.0 %copy-start.6 = (f32[1,128,128]{2,1,0:T(8,128)S(1)}, f32[1,128,128]{2,1,0:T(8,128)}, u32[]{:S(2)}) copy-start(f32[1,128,128]{2,1,0:T(8,128)} %param.17) | copy-start | bytes 196612
  10.0 72.2 %copy-start.1 = (f32[32,4096]{1,0:T(8,128)S(1)}, f32[32,4096]{1,0:T(8,128)}, u32[]{:S(2)}) copy-start(f32[32,4096]{1,0:T(8,128)} %param.19) | copy-start | bytes 1572868
  25.8 6.0 %copy-start.4 = (f32[128,32]{1,0:T(8,128)}, f32[128,32]{1,0:T(8,128)S(1)}, u32[]{:S(2)}) copy-start(f32[128,32]{1,0:T(8,128)S(1)} %convolution_bitcast_fusion.1) | copy-start | bytes 49156
  26.5 58.8 %collective-permute-start.2 = (f32[304,128]{1,0:T(8,128)}, f32[304,128]{1,0:T(8,128)}, u32[]{:S(2)}, u32[]{:S(2)}) collective-permute-start(f32[304,128]{1,0:T(8,128)} %select_maximum_fusion), channel_id=1, source_target_pairs={{3,4},{7,8},{11,12},{15,16},{19,20},{23,24},{27,28},{31,32},{35,36... | collective-permute-start | bytes 466952 | tf_op jit(solution)/shard_map/ppermute | solution.py:78
  89.1 0.7 copy-start.2

commit v5 on v4

--- a/solution.py
+++ b/solution.py
@@ -60,6 +60,7 @@
     groups = gathered[:, : at[1]].reshape(-1, nrhs)
     level2 = jnp.dot(level2_inverse[0], groups, precision=high)
     level3_in = jnp.dot(level2_basis[0], groups, precision=high)
+    level2, level3_in = lax.optimization_barrier((level2, level3_in))
 
     is_last = position == sub - 1
     n3 = level3_inverse.shape[1]
@@ -80,12 +81,12 @@
     gathered_in = level3_in
     for axis in ("core", "z", "x"):
         gathered_in = lax.all_gather(gathered_in, axis, axis=0, tiled=True)
+    incoming, gathered_in = lax.optimization_barrier((incoming, gathered_in))
     level3 = jnp.dot(level3_inverse, gathered_in, precision=high)
     corrected = level2 + jnp.dot(level2_basis[0].T, level3, precision=high)
     own_count = coarse.shape[0] * coarse.shape[1]
     own_rows = lax.dynamic_slice_in_dim(corrected, position * own_count, own_count, 0)
     per_sub = own_rows.reshape(coarse.shape[0], coarse.shape[1], -1)
-    update = local + jnp.einsum("snk,snr->srk", coarse_basis, per_sub, precision=high)
 
     cross_fold = incoming[: on[1]].reshape(nc, n3)
     cross_rows = incoming[on[3] : on[4], :nrhs]
@@ -110,7 +111,15 @@
     rims = rim_local + jnp.sum(rim_basis[:, :, None, :] * rim_coef[:, :, :, None], axis=1)
     from_before = rims[0:1]
     from_behind = rims[1:2]
-    return add_rims(update, from_before, from_behind)
+    lower = local[:, :, :IFW] + jnp.einsum("snk,snr->srk", coarse_basis[:, :, :IFW], per_sub, precision=high)
+    upper = local[:, :, nloc - IFW :] + jnp.einsum(
+        "snk,snr->srk", coarse_basis[:, :, nloc - IFW :], per_sub, precision=high)
+    prev_rims = jnp.concatenate([from_before, upper[:-1]], 0)
+    next_rims = jnp.concatenate([lower[1:], from_behind], 0)
+    middle = jnp.zeros((local.shape[0], nrhs, nloc - 2 * IFW), jnp.float32)
+    rim_terms = jnp.concatenate([0.5 * prev_rims, middle, 0.5 * next_rims], 2)
+    update = local + jnp.einsum("snk,snr->srk", coarse_basis, per_sub, precision=high)
+    return update + rim_terms
 
 
 def solution(mesh):

time: 91.9 us -> 97.4 us (1.060)
  the two profiles are of different devices: /device:TPU:24 before, /device:TPU:1 now
where the time goes in v5:
time: 97.4 us; the launch traced here: 96.6 us
  blocking collectives  57 us (59%)
  starting transfers between devices  18.2 us (19%)
  matrix products  10.6 us (11%)
  other arithmetic  6.1 us (6%)
  local copies, waits for them, and re-layouts  4.45 us (5%)
    all_gather x3, blocking collectives, shards(): gathered_in = lax.all_gather(gathered_in, axis, axis=0, tiled=True)  46.1 us
    all_gather x1, blocking collectives, shards(): gathered = lax.all_gather(packed, 'sub', axis=0, tiled=False)  10.9 us
    ppermute x1, starting transfers between devices, shards(): incoming = lax.ppermute(outgoing, SPREAD, pairs)  10.3 us
    ppermute x2, starting transfers between devices, from_behind_2(): return lax.ppermute(array, axis, pairs)  7.94 us
    dot_general x1, matrix products, shards(): jnp.einsum('snk,snr->srk', coarse_basis, per_sub, precision=high)  1.99 us
  transfers between devices with their start and end apart: 3, of which 0 were waited for; matrix products, arithmetic and copies ran while one was open for 3% of the time, Pallas kernels for 0%

profile of v5, /device:TPU:1, one launch (start us, length us, event | category | flops | bytes accessed | tf_op | source)
XLA Modules:
  0.0 96.6 jit_solution(5750486902699958331)
XLA Ops:
  0.0 1.1 %copy.31 = f32[4,32,512]{2,1,0:T(8,128)S(1)} copy(f32[4,32,512]{2,1,0:T(8,128)} %param.10) | data formatting | bytes 524288
  1.1 4.0 %collective-permute-start = (f32[1,32,128]{2,1,0:T(8,128)S(1)}, f32[1,32,128]{2,1,0:T(8,128)S(1)}, u32[]{:S(2)}, u32[]{:S(2)}) collective-permute-start(f32[1,32,128]{2,1,0:T(8,128)S(1)} %get-tuple-element.48), channel_id=1, source_target_pairs={{0,1},{1,2},{2,3},{3,4},{4,5},{5,6},{6,7},{7,8},{8,9},{9,10},{10,1... | collective-permute-start | bytes 49160 | tf_op jit(solution)/shard_map/ppermute | solution.py:13
  5.1 3.9 %collective-permute-start.1 = (f32[1,32,128]{2,1,0:T(8,128)S(1)}, f32[1,32,128]{2,1,0:T(8,128)S(1)}, u32[]{:S(2)}, u32[]{:S(2)}) collective-permute-start(f32[1,32,128]{2,1,0:T(8,128)S(1)} %get-tuple-element.47), channel_id=1, source_target_pairs={{1,0},{2,1},{3,2},{4,3},{5,4},{6,5},{7,6},{8,7},{9,8},{10,9},{11,1... | collective-permute-start | bytes 49160 | tf_op jit(solution)/shard_map/ppermute | solution.py:13
  9.1 1.6 %fusion.12 = f32[8,4096]{1,0:T(8,128)S(1)} fusion(f32[32,4096]{1,0:T(8,128)} %param.15, f32[32,128]{1,0:T(8,128)} %bitcast.95, pred[]{:T(512)S(6)} %eq.6), kind=kOutput, calls=%fused_computation.31 | convolution fusion | flops 12583168 | bytes 688129 | tf_op jit(solution)/shard_map/dot_general | solution.py:68
  10.7 0.7 reshape.83
  12.0 0.7 fusion.2
  15.0 10.9 %all-gather = f32[352,128]{1,0:T(8,128)} all-gather(f32[88,128]{1,0:T(8,128)S(1)} %get-tuple-element.52), channel_id=2, replica_groups=mesh['x'=4,'z'=16,'core'=2,'sub'=4] {'sub'}, dimensions={0}, use_global_device_ids=true | all-gather | bytes 225280 | tf_op jit(solution)/shard_map/all_gather | solution.py:59
  25.9 0.7 slice.193
  27.0 0.8 convolution_bitcast_fusion.1
  27.9 6.3 %all_gather.17 = f32[64,32]{1,0:T(8,128)S(1)} all-gather(f32[32,32]{1,0:T(8,128)S(1)} %copy.18), channel_id=1, replica_groups=mesh['x'=4,'z'=16,'core'=2,'sub'=4] {'core'}, dimensions={0}, use_global_device_ids=true | all-gather | bytes 12288 | tf_op jit(solution)/shard_map/all_gather | solution.py:83
  34.3 27.9 %all-gather.1 = f32[16,64,32]{1,2,0:T(8,128)S(1)} all-gather(f32[1,64,32]{1,2,0:T(8,128)S(1)} %copy.19), channel_id=1, replica_groups=mesh['x'=4,'z'=16,'core'=2,'sub'=4] {'z'}, dimensions={0}, use_global_device_ids=true | all-gather | bytes 139264 | tf_op jit(solution)/shard_map/all_gather | solution.py:83
  62.4 0.7 slice_select_fusion.2
  63.1 0.9 select_maximum_fusion
  64.1 10.3 %collective-permute-start.2 = (f32[304,128]{1,0:T(8,128)S(1)}, f32[304,128]{1,0:T(8,128)S(1)}, u32[]{:S(2)}, u32[]{:S(2)}) collective-permute-start(f32[304,128]{1,0:T(8,128)S(1)} %select_maximum_fusion), channel_id=1, source_target_pairs={{3,4},{7,8},{11,12},{15,16},{19,20},{23,24},{27,28},{31,32},{35,36... | collective-permute-start | bytes 466952 | tf_op jit(solution)/shard_map/ppermute | solution.py:79
  74.3 11.9 %all_gather.19 = f32[4096,32]{0,1:T(8,128)S(1)} all-gather(f32[1024,32]{0,1:T(8,128)S(1)} %reshape.88), channel_id=1, replica_groups=mesh['x'=4,'z'=16,'core'=2,'sub'=4] {'x'}, dimensions={0}, use_global_device_ids=true | all-gather | bytes 655360 | tf_op jit(solution)/shard_map/all_gather | solution.py:83
  86.8 1.1 %fusion.1 = f32[128,32]{1,0:T(8,128)S(1)} fusion(f32[128,32]{1,0:T(8,128)} %convolution_bitcast_fusion.1, f32[32,32]{1,0:T(8,128)S(1)} %fusion.41, f32[1,32,128]{2,1,0:T(8,128)S(1)} %copy-done.4), kind=kOutput, calls=%fused_computation.3 | convolution fusion | flops 1576960 | bytes 53248 | tf_op jit(solution)/shard_map/dot_general | solution.py:86
  88.0 1.0 %fusion.14 = f32[4,32,128]{2,1,0:T(8,128)S(1)} fusion(f32[4,8,512]{2,1,0:T(8,128)} %param.12, f32[128,32]{1,0:T(8,128)S(1)} %fusion.1, s32[]{:T(128)S(6)} %select_n.84), kind=kOutput, calls=%fused_computation.35 | convolution fusion | flops 1572864 | bytes 98308 | tf_op jit(solution)/shard_map/snk,snr->srk/dot_general | solution.py:114
  89.0 1.0 %fusion.16 = f32[4,32,128]{2,1,0:T(8,128)S(1)} fusion(f32[4,8,512]{2,1,0:T(8,128)} %param.12, f32[128,32]{1,0:T(8,128)S(1)} %fusion.1, s32[]{:T(128)S(6)} %select_n.84), kind=kOutput, calls=%fused_computation.37 | convolution fusion | flops 1572864 | bytes 98308 | tf_op jit(solution)/shard_map/snk,snr->srk/dot_general | solution.py:115
  90.1 0.8 fusion.11
  90.9 0.7 fusion.31
  91.6 1.2 %select_bitcast_fusion.1 = (f32[1,8,32]{2,1,0:T(8,128)S(1)}, f32[1,8,32]{2,1,0:T(8,128)S(1)}) fusion(f32[128,32]{1,0:T(8,128)S(1)} %fusion.1, s32[]{:T(128)S(6)} %select_n.93, pred[]{:T(512)S(6)} %eq.7, f32[304,128]{1,0:T(8,128)} %copy-done.3, s32[]{:T(128)S(6)} %select_n.95, pred[]{:T(512)S(6)} %eq.6, f32[8,4096]{1,0:T(8,128)S(1)} %reshape.85, ...), kind=kOutput, calls=%fused_computation.62 | convolution fusion | flops 12583680 | bytes 660490 | tf_op jit(solution)/shard_map/dot_general | solution.py:93
  93.0 0.8 slice_add_fusion.1
  93.8 0.8 slice_add_fusion.2
  94.6 2.0 %fusion = f32[4,32,512]{2,1,0:T(8,128)} fusion(f32[4,32,512]{2,1,0:T(8,128)S(1)} %fusion.2, f32[4,8,512]{2,1,0:T(8,128)} %param.12, f32[4,32,128]{2,1,0:T(8,128)S(1)} %get-tuple-element.56, f32[4,32,128]{2,1,0:T(8,128)S(1)} %get-tuple-element.55, f32[512]{0:T(512)} %pad.10.clone, f32[128,32]{1,0:T(8,128)S(1)} %fusion.1, s32[]{:T(128)S(6)} %select_n.84), kind=kOutput, calls=%fused_computation.1 | convolution fusion | flops 6553600 | bytes 739332 | tf_op jit(solution)/shard_map/snk,snr->srk/dot_general | solution.py:121
  (44 shorter events, 4.5 us)
Async XLA Ops:
  0.0 12.0 %copy-start = (bf16[4,512,512]{2,1,0:T(8,128)(2,1)S(1)}, bf16[4,512,512]{2,1,0:T(8,128)(2,1)}, u32[]{:S(2)}) copy-start(bf16[4,512,512]{2,1,0:T(8,128)(2,1)} %param.11) | copy-start | bytes 6291460
  1.1 10.8 %collective-permute-start = (f32[1,32,128]{2,1,0:T(8,128)S(1)}, f32[1,32,128]{2,1,0:T(8,128)S(1)}, u32[]{:S(2)}, u32[]{:S(2)}) collective-permute-start(f32[1,32,128]{2,1,0:T(8,128)S(1)} %get-tuple-element.48), channel_id=1, source_target_pairs={{0,1},{1,2},{2,3},{3,4},{4,5},{5,6},{6,7},{7,8},{8,9},{9,10},{10,1... | collective-permute-start | bytes 49160 | tf_op jit(solution)/shard_map/ppermute | solution.py:13
  5.1 6.8 %collective-permute-start.1 = (f32[1,32,128]{2,1,0:T(8,128)S(1)}, f32[1,32,128]{2,1,0:T(8,128)S(1)}, u32[]{:S(2)}, u32[]{:S(2)}) collective-permute-start(f32[1,32,128]{2,1,0:T(8,128)S(1)} %get-tuple-element.47), channel_id=1, source_target_pairs={{1,0},{2,1},{3,2},{4,3},{5,4},{6,5},{7,6},{8,7},{9,8},{10,9},{11,1... | collective-permute-start | bytes 49160 | tf_op jit(solution)/shard_map/ppermute | solution.py:13
  9.1 3.7 %copy-start.2 = (f32[4,8,512]{2,1,0:T(8,128)S(1)}, f32[4,8,512]{2,1,0:T(8,128)}, u32[]{:S(2)}) copy-start(f32[4,8,512]{2,1,0:T(8,128)} %param.12) | copy-start | bytes 196612
  11.4 15.4 %copy-start.4 = (f32[1,32,128]{2,1,0:T(8,128)S(1)}, f32[1,32,128]{2,1,0:T(8,128)}, u32[]{:S(2)}) copy-start(f32[1,32,128]{2,1,0:T(8,128)} %param.14) | copy-start | bytes 49156
  11.9 15.0 %copy-start.5 = (f32[1,128,128]{2,1,0:T(8,128)S(1)}, f32[1,128,128]{2,1,0:T(8,128)}, u32[]{:S(2)}) copy-start(f32[1,128,128]{2,1,0:T(8,128)} %param.13) | copy-start | bytes 196612
  12.7 73.6 %copy-start.1 = (f32[32,4096]{1,0:T(8,128)S(1)}, f32[32,4096]{1,0:T(8,128)}, u32[]{:S(2)}) copy-start(f32[32,4096]{1,0:T(8,128)} %param.15) | copy-start | bytes 1572868
  64.1 22.2 %collective-permute-start.2 = (f32[304,128]{1,0:T(8,128)S(1)}, f32[304,128]{1,0:T(8,128)S(1)}, u32[]{:S(2)}, u32[]{:S(2)}) collective-permute-start(f32[304,128]{1,0:T(8,128)S(1)} %select_maximum_fusion), channel_id=1, source_target_pairs={{3,4},{7,8},{11,12},{15,16},{19,20},{23,24},{27,28},{31,32},{35,36... | collective-permute-start | bytes 466952 | tf_op jit(solution)/shard_map/ppermute | solution.py:79
  86.3 3.8 %copy-start.3 = (f32[304,128]{1,0:T(8,128)}, f32[304,128]{1,0:T(8,128)S(1)}, u32[]{:S(2)}) copy-start(f32[304,128]{1,0:T(8,128)S(1)} %collective-permute-done.2) | copy-start | bytes 466948

commit v6 on v4

--- a/solution.py
+++ b/solution.py
@@ -31,12 +31,12 @@
 
 
 def rim_update(local_rim, basis_rim, coefficients):
-    high = lax.Precision.HIGHEST
+    high = lax.Precision.HIGH
     return local_rim + jnp.einsum("snk,snr->srk", basis_rim, coefficients[None], precision=high)
 
 
 def shards(residual_in, local_inverse, coarse_basis, level2_inverse, level2_basis, level3_inverse):
-    high = lax.Precision.HIGHEST
+    high = lax.Precision.HIGH
     sub = lax.axis_size("sub")
     position = lax.axis_index("sub")
     nloc = residual_in.shape[2]

time: 91.9 us -> 91 us (level)
  no operation moved by 1% of the time
where the time goes in v6:
time: 91 us; the launch traced here: 90.4 us
  blocking collectives  67.3 us (74%)
  starting transfers between devices  7.74 us (9%)
  matrix products  6.39 us (7%)
  local copies, waits for them, and re-layouts  4.14 us (5%)
  other arithmetic  3.85 us (4%)
    all_gather x3, blocking collectives, shards(): gathered_in = lax.all_gather(gathered_in, axis, axis=0, tiled=True)  53.4 us
    all_gather x1, blocking collectives, shards(): gathered = lax.all_gather(packed, 'sub', axis=0, tiled=False)  13.9 us
    ppermute x2, starting transfers between devices, from_behind_2(): return lax.ppermute(array, axis, pairs)  5.83 us
    unnamed x19, local copies, waits for them, and re-layouts  2.04 us
    ppermute x1, starting transfers between devices, shards(): incoming = lax.ppermute(outgoing, SPREAD, pairs)  1.91 us
  transfers between devices with their start and end apart: 3, of which 1 were waited for; matrix products, arithmetic and copies ran while one was open for 5% of the time, Pallas kernels for 0%

profile of v6, /device:TPU:24, one launch (start us, length us, event | category | flops | bytes accessed | tf_op | source)
XLA Modules:
  0.0 90.4 jit_solution(4209521532330038491)
XLA Ops:
  0.0 1.1 %copy.33 = f32[4,32,512]{2,1,0:T(8,128)S(1)} copy(f32[4,32,512]{2,1,0:T(8,128)} %param.14) | data formatting | bytes 524288
  1.1 1.9 %collective-permute-start = (f32[1,32,128]{2,1,0:T(8,128)S(1)}, f32[1,32,128]{2,1,0:T(8,128)S(1)}, u32[]{:S(2)}, u32[]{:S(2)}) collective-permute-start(f32[1,32,128]{2,1,0:T(8,128)S(1)} %get-tuple-element.64), channel_id=1, source_target_pairs={{0,1},{1,2},{2,3},{3,4},{4,5},{5,6},{6,7},{7,8},{8,9},{9,10},{10,1... | collective-permute-start | bytes 49160 | tf_op jit(solution)/shard_map/ppermute | solution.py:13
  3.0 3.9 %collective-permute-start.1 = (f32[1,32,128]{2,1,0:T(8,128)S(1)}, f32[1,32,128]{2,1,0:T(8,128)S(1)}, u32[]{:S(2)}, u32[]{:S(2)}) collective-permute-start(f32[1,32,128]{2,1,0:T(8,128)S(1)} %get-tuple-element.63), channel_id=1, source_target_pairs={{1,0},{2,1},{3,2},{4,3},{5,4},{6,5},{7,6},{8,7},{9,8},{10,9},{11,1... | collective-permute-start | bytes 49160 | tf_op jit(solution)/shard_map/ppermute | solution.py:13
  7.0 1.5 %fusion.13 = f32[8,4096]{1,0:T(8,128)S(1)} fusion(f32[32,4096]{1,0:T(8,128)} %param.19, f32[32,128]{1,0:T(8,128)} %bitcast.91, pred[]{:T(512)S(6)} %eq.7), kind=kOutput, calls=%fused_computation.32 | convolution fusion | flops 6291712 | bytes 688129 | tf_op jit(solution)/shard_map/dot_general | solution.py:67
  8.6 0.7 collective-permute-done.1
  9.3 0.7 fusion.1
  10.1 0.2 convolution_bitcast_fusion.3
  10.4 13.9 %all-gather = f32[352,128]{1,0:T(8,128)} all-gather(f32[88,128]{1,0:T(8,128)S(1)} %constant_dynamic-update-slice_fusion), channel_id=2, replica_groups=mesh['x'=4,'z'=16,'core'=2,'sub'=4] {'sub'}, dimensions={0}, use_global_device_ids=true | all-gather | bytes 225280 | tf_op jit(solution)/shard_map/all_gather | solution.py:59
  24.3 0.7 slice.231
  25.1 0.2 convolution_bitcast_fusion.2
  25.6 0.7 select_maximum_fusion
  26.3 1.9 %collective-permute-start.2 = (f32[304,128]{1,0:T(8,128)}, f32[304,128]{1,0:T(8,128)}, u32[]{:S(2)}, u32[]{:S(2)}) collective-permute-start(f32[304,128]{1,0:T(8,128)} %select_maximum_fusion), channel_id=1, source_target_pairs={{3,4},{7,8},{11,12},{15,16},{19,20},{23,24},{27,28},{31,32},{35,36... | collective-permute-start | bytes 466952 | tf_op jit(solution)/shard_map/ppermute | solution.py:78
  28.2 3.2 %all_gather.17 = f32[64,32]{1,0:T(8,128)S(1)} all-gather(f32[32,32]{1,0:T(8,128)S(1)} %copy.18), channel_id=1, replica_groups=mesh['x'=4,'z'=16,'core'=2,'sub'=4] {'core'}, dimensions={0}, use_global_device_ids=true | all-gather | bytes 12288 | tf_op jit(solution)/shard_map/all_gather | solution.py:82
  31.5 37.0 %all-gather.1 = f32[16,64,32]{1,2,0:T(8,128)S(1)} all-gather(f32[1,64,32]{1,2,0:T(8,128)S(1)} %copy.19), channel_id=1, replica_groups=mesh['x'=4,'z'=16,'core'=2,'sub'=4] {'z'}, dimensions={0}, use_global_device_ids=true | all-gather | bytes 139264 | tf_op jit(solution)/shard_map/all_gather | solution.py:82
  68.8 13.1 %all_gather.19 = f32[4096,32]{0,1:T(8,128)S(1)} all-gather(f32[1024,32]{0,1:T(8,128)S(1)} %reshape.144), channel_id=1, replica_groups=mesh['x'=4,'z'=16,'core'=2,'sub'=4] {'x'}, dimensions={0}, use_global_device_ids=true | all-gather | bytes 655360 | tf_op jit(solution)/shard_map/all_gather | solution.py:82
  82.0 0.4 fusion.32
  82.3 1.1 %fusion = f32[128,32]{1,0:T(8,128)S(1)} fusion(f32[128,32]{1,0:T(8,128)} %copy-done.4, f32[32,32]{1,0:T(8,128)S(1)} %fusion.32, f32[1,32,128]{2,1,0:T(8,128)S(1)} %copy-done.5), kind=kOutput, calls=%fused_computation.2 | convolution fusion | flops 790528 | bytes 53248 | tf_op jit(solution)/shard_map/dot_general | solution.py:84
  83.4 1.2 %convolution_add_fusion = f32[4,32,512]{2,1,0:T(8,128)S(1)} fusion(f32[4,32,512]{2,1,0:T(8,128)S(1)} %fusion.1, f32[4,8,512]{2,1,0:T(8,128)} %param.16, f32[128,32]{1,0:T(8,128)S(1)} %fusion, s32[]{:T(128)S(6)} %select_n.76), kind=kOutput, calls=%fused_computation | convolution fusion | flops 3211264 | bytes 606212 | tf_op jit(solution)/shard_map/snk,snr->srk/dot_general | solution.py:88
  84.6 0.9 %slice.240 = f32[256,128]{1,0:T(8,128)S(1)} slice(f32[304,128]{1,0:T(8,128)} %collective-permute-done.2), slice={[0:256], [0:128]} | slice | bytes 262144 | tf_op jit(solution)/shard_map/slice | solution.py:90
  85.6 0.7 fusion.24
  86.3 1.0 %select_bitcast_fusion.1 = (f32[1,8,32]{2,1,0:T(8,128)S(1)}, f32[1,8,32]{2,1,0:T(8,128)S(1)}) fusion(f32[128,32]{1,0:T(8,128)S(1)} %fusion, s32[]{:T(128)S(6)} %select_n.93, pred[]{:T(512)S(6)} %eq.6, f32[304,128]{1,0:T(8,128)} %collective-permute-done.2, s32[]{:T(128)S(6)} %select_n.95, pred[]{:T(512)S(6)} %eq.7, f32[8,4096]{1,0:T(8,128)S(1)} %reshape.141, ...), kind=kOutput, calls=%fused_computation.57 | convolution fusion | flops 6292224 | bytes 660490 | tf_op jit(solution)/shard_map/dot_general | solution.py:92
  87.4 0.8 fusion.12
  88.3 0.7 copy-done.2
  89.0 1.5 %fusion.3 = f32[4,32,512]{2,1,0:T(8,128)} fusion(f32[4,32,512]{2,1,0:T(8,128)} %copy-done.2, f32[1,32,128]{2,1,0:T(8,128)S(1)} %get-tuple-element.69, f32[3,32,128]{2,1,0:T(8,128)S(1)} %get-tuple-element.57), kind=kLoop, calls=%fused_computation.12 | loop fusion | flops 49152 | bytes 196608 | tf_op jit(solution)/shard_map/scatter-add | solution.py:30
  (41 shorter events, 1.1 us)
Async XLA Ops:
  0.0 9.3 %copy-start = (bf16[4,512,512]{2,1,0:T(8,128)(2,1)S(1)}, bf16[4,512,512]{2,1,0:T(8,128)(2,1)}, u32[]{:S(2)}) copy-start(bf16[4,512,512]{2,1,0:T(8,128)(2,1)} %param.15) | copy-start | bytes 6291460
  1.1 7.4 %collective-permute-start = (f32[1,32,128]{2,1,0:T(8,128)S(1)}, f32[1,32,128]{2,1,0:T(8,128)S(1)}, u32[]{:S(2)}, u32[]{:S(2)}) collective-permute-start(f32[1,32,128]{2,1,0:T(8,128)S(1)} %get-tuple-element.64), channel_id=1, source_target_pairs={{0,1},{1,2},{2,3},{3,4},{4,5},{5,6},{6,7},{7,8},{8,9},{9,10},{10,1... | collective-permute-start | bytes 49160 | tf_op jit(solution)/shard_map/ppermute | solution.py:13
  3.0 6.3 %collective-permute-start.1 = (f32[1,32,128]{2,1,0:T(8,128)S(1)}, f32[1,32,128]{2,1,0:T(8,128)S(1)}, u32[]{:S(2)}, u32[]{:S(2)}) collective-permute-start(f32[1,32,128]{2,1,0:T(8,128)S(1)} %get-tuple-element.63), channel_id=1, source_target_pairs={{1,0},{2,1},{3,2},{4,3},{5,4},{6,5},{7,6},{8,7},{9,8},{10,9},{11,1... | collective-permute-start | bytes 49160 | tf_op jit(solution)/shard_map/ppermute | solution.py:13
  7.0 3.1 %copy-start.3 = (f32[4,8,512]{2,1,0:T(8,128)S(1)}, f32[4,8,512]{2,1,0:T(8,128)}, u32[]{:S(2)}) copy-start(f32[4,8,512]{2,1,0:T(8,128)} %param.16) | copy-start | bytes 196612
  8.5 16.7 %copy-start.5 = (f32[1,32,128]{2,1,0:T(8,128)S(1)}, f32[1,32,128]{2,1,0:T(8,128)}, u32[]{:S(2)}) copy-start(f32[1,32,128]{2,1,0:T(8,128)} %param.18) | copy-start | bytes 49156
  8.5 16.9 %copy-start.6 = (f32[1,128,128]{2,1,0:T(8,128)S(1)}, f32[1,128,128]{2,1,0:T(8,128)}, u32[]{:S(2)}) copy-start(f32[1,128,128]{2,1,0:T(8,128)} %param.17) | copy-start | bytes 196612
  10.0 71.9 %copy-start.1 = (f32[32,4096]{1,0:T(8,128)S(1)}, f32[32,4096]{1,0:T(8,128)}, u32[]{:S(2)}) copy-start(f32[32,4096]{1,0:T(8,128)} %param.19) | copy-start | bytes 1572868
  25.6 6.0 %copy-start.4 = (f32[128,32]{1,0:T(8,128)}, f32[128,32]{1,0:T(8,128)S(1)}, u32[]{:S(2)}) copy-start(f32[128,32]{1,0:T(8,128)S(1)} %convolution_bitcast_fusion.1) | copy-start | bytes 49156
  26.3 58.4 %collective-permute-start.2 = (f32[304,128]{1,0:T(8,128)}, f32[304,128]{1,0:T(8,128)}, u32[]{:S(2)}, u32[]{:S(2)}) collective-permute-start(f32[304,128]{1,0:T(8,128)} %select_maximum_fusion), channel_id=1, source_target_pairs={{3,4},{7,8},{11,12},{15,16},{19,20},{23,24},{27,28},{31,32},{35,36... | collective-permute-start | bytes 466952 | tf_op jit(solution)/shard_map/ppermute | solution.py:78
  88.3 0.7 copy-start.2

commit v7 on v6

--- a/solution.py
+++ b/solution.py
@@ -43,7 +43,15 @@
     nc = coarse_basis.shape[1]
     rhs = couple(residual_in)
     rhs_low = rhs.astype(jnp.bfloat16)
-    local = jnp.einsum("srk,sjk->srj", rhs_low, local_inverse, preferred_element_type=jnp.float32)
+    inner = residual_in[1:-1]
+    inner = inner.at[:, :, :IFW].add(0.5 * residual_in[:-2, :, nloc - IFW :])
+    inner = inner.at[:, :, nloc - IFW :].add(0.5 * residual_in[2:, :, :IFW])
+    inner_local = jnp.einsum(
+        "srk,sjk->srj", inner.astype(jnp.bfloat16), local_inverse[1:-1], preferred_element_type=jnp.float32)
+    edge_local = jnp.einsum(
+        "srk,sjk->srj", rhs_low[::residual_in.shape[0] - 1], local_inverse[::residual_in.shape[0] - 1],
+        preferred_element_type=jnp.float32)
+    local = jnp.concatenate([edge_local[:1], inner_local, edge_local[1:]], 0)
     coarse = jnp.einsum("snk,srk->snr", coarse_basis, rhs, precision=high)
     nrhs = local.shape[1]
 

time: 91 us -> 84.9 us (0.933)
  matrix products: 6.39 us -> 4.3 us
  other arithmetic: 3.85 us -> 1.78 us
  local copies, waits for them, and re-layouts: 4.14 us -> 3.15 us
    dot_general x1 -> x2, matrix products: 0.71 us -> 2.06 us  [the longest x1 1.66 us: shards(): jnp.einsum('srk,sjk->srj', inner.astype(jnp.bfloat16), local_inverse[1:-1...]
    dot_general x1, matrix products: 1.46 us -> 0.35 us  [shards(): fold = jnp.dot(pick.T, level3_inverse, precision=high)]
    unnamed x19 -> x17, local copies, waits for them, and re-layouts: 2.04 us -> 2.03 us
  transfers between devices with their start and end apart: 3 -> 3, of which waited for: 1 -> 1; matrix products, arithmetic and copies ran while one was open for 5% -> 4% of each run, Pallas kernels for 0% -> 0%
where the time goes in v7:
time: 84.9 us; the launch traced here: 84.7 us
  blocking collectives  67 us (79%)
  starting transfers between devices  7.75 us (9%)
  matrix products  4.3 us (5%)
  local copies, waits for them, and re-layouts  3.15 us (4%)
  other arithmetic  1.78 us (2%)
    all_gather x3, blocking collectives, shards(): gathered_in = lax.all_gather(gathered_in, axis, axis=0, tiled=True)  53.3 us
    all_gather x1, blocking collectives, shards(): gathered = lax.all_gather(packed, 'sub', axis=0, tiled=False)  13.6 us
    ppermute x2, starting transfers between devices, from_behind_2(): return lax.ppermute(array, axis, pairs)  5.83 us
    unnamed x17, local copies, waits for them, and re-layouts  2.03 us
    ppermute x1, starting transfers between devices, shards(): incoming = lax.ppermute(outgoing, SPREAD, pairs)  1.92 us
  transfers between devices with their start and end apart: 3, of which 1 were waited for; matrix products, arithmetic and copies ran while one was open for 4% of the time, Pallas kernels for 0%

profile of v7, /device:TPU:24, one launch (start us, length us, event | category | flops | bytes accessed | tf_op | source)
XLA Modules:
  0.0 84.7 jit_solution(8757924389609322804)
XLA Ops:
  0.0 1.1 %copy.35 = f32[4,32,512]{2,1,0:T(8,128)S(1)} copy(f32[4,32,512]{2,1,0:T(8,128)} %param.18) | data formatting | bytes 524288
  1.1 0.6 fusion.35
  1.7 1.9 %collective-permute-start = (f32[1,32,128]{2,1,0:T(8,128)}, f32[1,32,128]{2,1,0:T(8,128)S(1)}, u32[]{:S(2)}, u32[]{:S(2)}) collective-permute-start(f32[1,32,128]{2,1,0:T(8,128)} %get-tuple-element.86), channel_id=1, source_target_pairs={{0,1},{1,2},{2,3},{3,4},{4,5},{5,6},{6,7},{7,8},{8,9},{9,10},{10,1... | collective-permute-start | bytes 49160 | tf_op jit(solution)/shard_map/ppermute | solution.py:13
  3.6 3.9 %collective-permute-start.1 = (f32[1,32,128]{2,1,0:T(8,128)}, f32[1,32,128]{2,1,0:T(8,128)S(1)}, u32[]{:S(2)}, u32[]{:S(2)}) collective-permute-start(f32[1,32,128]{2,1,0:T(8,128)} %get-tuple-element.85), channel_id=1, source_target_pairs={{1,0},{2,1},{3,2},{4,3},{5,4},{6,5},{7,6},{8,7},{9,8},{10,9},{11,1... | collective-permute-start | bytes 49160 | tf_op jit(solution)/shard_map/ppermute | solution.py:13
  7.7 1.7 %fusion.1 = f32[2,32,512]{2,1,0:T(8,128)S(1)} fusion(bf16[4,512,512]{2,1,0:T(8,128)(2,1)} %param.19, f32[2,32,512]{2,1,0:T(8,128)S(1)} %fusion.13), kind=kOutput, calls=%fused_computation.6 | convolution fusion | flops 33587200 | bytes 1310720 | tf_op jit(solution)/shard_map/srk,sjk->srj/dot_general | solution.py:49
  9.3 0.3 fusion.18
  9.8 0.3 collective-permute-done.1
  10.2 0.4 fusion.3
  10.6 0.2 convolution_bitcast_fusion.3
  11.0 13.6 %all-gather = f32[352,128]{1,0:T(8,128)S(1)} all-gather(f32[88,128]{1,0:T(8,128)S(1)} %constant_dynamic-update-slice_fusion), channel_id=2, replica_groups=mesh['x'=4,'z'=16,'core'=2,'sub'=4] {'sub'}, dimensions={0}, use_global_device_ids=true | all-gather | bytes 225280 | tf_op jit(solution)/shard_map/all_gather | solution.py:67
  24.7 0.2 convolution_bitcast_fusion.2
  24.9 0.2 convolution_bitcast_fusion.1
  25.1 1.9 %collective-permute-start.2 = (f32[304,128]{1,0:T(8,128)S(1)}, f32[304,128]{1,0:T(8,128)S(1)}, u32[]{:S(2)}, u32[]{:S(2)}) collective-permute-start(f32[304,128]{1,0:T(8,128)S(1)} %select_maximum_fusion), channel_id=1, source_target_pairs={{3,4},{7,8},{11,12},{15,16},{19,20},{23,24},{27,28},{31,32},{35,36... | collective-permute-start | bytes 466952 | tf_op jit(solution)/shard_map/ppermute | solution.py:86
  27.1 3.3 %all_gather.17 = f32[64,32]{1,0:T(8,128)S(1)} all-gather(f32[32,32]{1,0:T(8,128)S(1)} %copy.18), channel_id=1, replica_groups=mesh['x'=4,'z'=16,'core'=2,'sub'=4] {'core'}, dimensions={0}, use_global_device_ids=true | all-gather | bytes 12288 | tf_op jit(solution)/shard_map/all_gather | solution.py:90
  30.5 37.0 %all-gather.1 = f32[16,64,32]{1,2,0:T(8,128)S(1)} all-gather(f32[1,64,32]{1,2,0:T(8,128)S(1)} %copy.19), channel_id=1, replica_groups=mesh['x'=4,'z'=16,'core'=2,'sub'=4] {'z'}, dimensions={0}, use_global_device_ids=true | all-gather | bytes 139264 | tf_op jit(solution)/shard_map/all_gather | solution.py:90
  67.4 0.2 copy.20
  67.7 13.1 %all_gather.19 = f32[4096,32]{0,1:T(8,128)S(1)} all-gather(f32[1024,32]{0,1:T(8,128)S(1)} %reshape.200), channel_id=1, replica_groups=mesh['x'=4,'z'=16,'core'=2,'sub'=4] {'x'}, dimensions={0}, use_global_device_ids=true | all-gather | bytes 655360 | tf_op jit(solution)/shard_map/all_gather | solution.py:90
  80.8 0.4 fusion.38
  81.2 0.2 fusion
  81.5 0.3 convolution_add_fusion
  81.9 0.3 select_bitcast_fusion.1
  82.3 0.1 multiply_reduce_fusion
  82.5 0.7 copy-done.2
  83.2 1.5 %fusion.5 = f32[4,32,512]{2,1,0:T(8,128)} fusion(f32[4,32,512]{2,1,0:T(8,128)} %copy-done.2, f32[1,32,128]{2,1,0:T(8,128)S(1)} %get-tuple-element.95, f32[3,32,128]{2,1,0:T(8,128)S(1)} %get-tuple-element.81), kind=kLoop, calls=%fused_computation.14 | loop fusion | flops 49152 | bytes 196608 | tf_op jit(solution)/shard_map/scatter-add | solution.py:30
  (45 shorter events, 0.8 us)
Async XLA Ops:
  0.0 9.3 %copy-start = (f32[32,4096]{1,0:T(8,128)S(1)}, f32[32,4096]{1,0:T(8,128)}, u32[]{:S(2)}) copy-start(f32[32,4096]{1,0:T(8,128)} %param.23) | copy-start | bytes 1572868
  0.0 10.2 %copy-start.1 = (bf16[4,512,512]{2,1,0:T(8,128)(2,1)S(1)}, bf16[4,512,512]{2,1,0:T(8,128)(2,1)}, u32[]{:S(2)}) copy-start(bf16[4,512,512]{2,1,0:T(8,128)(2,1)} %param.19) | copy-start | bytes 6291460
  0.0 9.3 %copy-start.4 = (f32[1,32,128]{2,1,0:T(8,128)S(1)}, f32[1,32,128]{2,1,0:T(8,128)}, u32[]{:S(2)}) copy-start(f32[1,32,128]{2,1,0:T(8,128)} %param.22) | copy-start | bytes 49156
  1.7 8.1 %collective-permute-start = (f32[1,32,128]{2,1,0:T(8,128)}, f32[1,32,128]{2,1,0:T(8,128)S(1)}, u32[]{:S(2)}, u32[]{:S(2)}) collective-permute-start(f32[1,32,128]{2,1,0:T(8,128)} %get-tuple-element.86), channel_id=1, source_target_pairs={{0,1},{1,2},{2,3},{3,4},{4,5},{5,6},{6,7},{7,8},{8,9},{9,10},{10,1... | collective-permute-start | bytes 49160 | tf_op jit(solution)/shard_map/ppermute | solution.py:13
  3.6 6.5 %collective-permute-start.1 = (f32[1,32,128]{2,1,0:T(8,128)}, f32[1,32,128]{2,1,0:T(8,128)S(1)}, u32[]{:S(2)}, u32[]{:S(2)}) collective-permute-start(f32[1,32,128]{2,1,0:T(8,128)} %get-tuple-element.85), channel_id=1, source_target_pairs={{1,0},{2,1},{3,2},{4,3},{5,4},{6,5},{7,6},{8,7},{9,8},{10,9},{11,1... | collective-permute-start | bytes 49160 | tf_op jit(solution)/shard_map/ppermute | solution.py:13
  7.6 2.9 %copy-start.3 = (f32[4,8,512]{2,1,0:T(8,128)S(1)}, f32[4,8,512]{2,1,0:T(8,128)}, u32[]{:S(2)}) copy-start(f32[4,8,512]{2,1,0:T(8,128)} %param.20) | copy-start | bytes 196612
  9.3 15.6 %copy-start.5 = (f32[1,128,128]{2,1,0:T(8,128)S(1)}, f32[1,128,128]{2,1,0:T(8,128)}, u32[]{:S(2)}) copy-start(f32[1,128,128]{2,1,0:T(8,128)} %param.21) | copy-start | bytes 196612
  25.1 56.7 %collective-permute-start.2 = (f32[304,128]{1,0:T(8,128)S(1)}, f32[304,128]{1,0:T(8,128)S(1)}, u32[]{:S(2)}, u32[]{:S(2)}) collective-permute-start(f32[304,128]{1,0:T(8,128)S(1)} %select_maximum_fusion), channel_id=1, source_target_pairs={{3,4},{7,8},{11,12},{15,16},{19,20},{23,24},{27,28},{31,32},{35,36... | collective-permute-start | bytes 466952 | tf_op jit(solution)/shard_map/ppermute | solution.py:86
  82.5 0.7 copy-start.2

commit v8 on v7

--- a/solution.py
+++ b/solution.py
@@ -68,6 +68,7 @@
     groups = gathered[:, : at[1]].reshape(-1, nrhs)
     level2 = jnp.dot(level2_inverse[0], groups, precision=high)
     level3_in = jnp.dot(level2_basis[0], groups, precision=high)
+    level2, level3_in = lax.optimization_barrier((level2, level3_in))
 
     is_last = position == sub - 1
     n3 = level3_inverse.shape[1]
@@ -88,12 +89,12 @@
     gathered_in = level3_in
     for axis in ("core", "z", "x"):
         gathered_in = lax.all_gather(gathered_in, axis, axis=0, tiled=True)
+    incoming, gathered_in = lax.optimization_barrier((incoming, gathered_in))
     level3 = jnp.dot(level3_inverse, gathered_in, precision=high)
     corrected = level2 + jnp.dot(level2_basis[0].T, level3, precision=high)
     own_count = coarse.shape[0] * coarse.shape[1]
     own_rows = lax.dynamic_slice_in_dim(corrected, position * own_count, own_count, 0)
     per_sub = own_rows.reshape(coarse.shape[0], coarse.shape[1], -1)
-    update = local + jnp.einsum("snk,snr->srk", coarse_basis, per_sub, precision=high)
 
     cross_fold = incoming[: on[1]].reshape(nc, n3)
     cross_rows = incoming[on[3] : on[4], :nrhs]
@@ -118,7 +119,15 @@
     rims = rim_local + jnp.sum(rim_basis[:, :, None, :] * rim_coef[:, :, :, None], axis=1)
     from_before = rims[0:1]
     from_behind = rims[1:2]
-    return add_rims(update, from_before, from_behind)
+    lower = local[:, :, :IFW] + jnp.einsum("snk,snr->srk", coarse_basis[:, :, :IFW], per_sub, precision=high)
+    upper = local[:, :, nloc - IFW :] + jnp.einsum(
+        "snk,snr->srk", coarse_basis[:, :, nloc - IFW :], per_sub, precision=high)
+    prev_rims = jnp.concatenate([from_before, upper[:-1]], 0)
+    next_rims = jnp.concatenate([lower[1:], from_behind], 0)
+    middle = jnp.zeros((local.shape[0], nrhs, nloc - 2 * IFW), jnp.float32)
+    rim_terms = jnp.concatenate([0.5 * prev_rims, middle, 0.5 * next_rims], 2)
+    update = local + jnp.einsum("snk,snr->srk", coarse_basis, per_sub, precision=high)
+    return update + rim_terms
 
 
 def solution(mesh):

time: 84.9 us -> 87 us (1.025); the launches traced: 84.7 us -> 85.5 us
  starting transfers between devices: 7.75 us -> 10.7 us
  other arithmetic: 1.78 us -> 0.34 us
  blocking collectives: 67 us -> 65.7 us
  matrix products: 4.3 us -> 5.46 us
    all_gather x3, blocking collectives: 53.3 us -> 51 us  [shards(): gathered_in = lax.all_gather(gathered_in, axis, axis=0, tiled=True)]
    ppermute x1, starting transfers between devices: 1.92 us -> 3.76 us  [shards(): incoming = lax.ppermute(outgoing, SPREAD, pairs)]
    scatter-add x2 -> x1, other arithmetic: 1.49 us -> 0.02 us  [add_rims(): return coupled.at[:, :, values_in.shape[2] - IFW:].add(0.5 * next_rims)]
    ppermute x2, starting transfers between devices: 5.83 us -> 6.89 us  [from_behind_2(): return lax.ppermute(array, axis, pairs)]
    all_gather x1, blocking collectives: 13.6 us -> 14.7 us  [shards(): gathered = lax.all_gather(packed, 'sub', axis=0, tiled=False)]
    unnamed x17 -> x18, local copies, waits for them, and re-layouts: 2.03 us -> 1.25 us
  transfers between devices with their start and end apart: 3 -> 3, of which waited for: 1 -> 0; matrix products, arithmetic and copies ran while one was open for 4% -> 3% of each run, Pallas kernels for 0% -> 0%
where the time goes in v8:
time: 87 us; the launch traced here: 85.5 us
  blocking collectives  65.7 us (76%)
  starting transfers between devices  10.7 us (12%)
  matrix products  5.46 us (6%)
  local copies, waits for them, and re-layouts  2.97 us (3%)
    all_gather x3, blocking collectives, shards(): gathered_in = lax.all_gather(gathered_in, axis, axis=0, tiled=True)  51 us
    all_gather x1, blocking collectives, shards(): gathered = lax.all_gather(packed, 'sub', axis=0, tiled=False)  14.7 us
    ppermute x2, starting transfers between devices, from_behind_2(): return lax.ppermute(array, axis, pairs)  6.89 us
    ppermute x1, starting transfers between devices, shards(): incoming = lax.ppermute(outgoing, SPREAD, pairs)  3.76 us
  transfers between devices with their start and end apart: 3, of which 0 were waited for; matrix products, arithmetic and copies ran while one was open for 3% of the time, Pallas kernels for 0%

profile of v8, /device:TPU:24, one launch (start us, length us, event | category | flops | bytes accessed | tf_op | source)
XLA Modules:
  0.0 85.5 jit_solution(14522631749359583156)
XLA Ops:
  0.0 1.0 %copy.33 = f32[4,32,512]{2,1,0:T(8,128)S(1)} copy(f32[4,32,512]{2,1,0:T(8,128)} %param.14) | data formatting | bytes 524288
  1.0 0.6 fusion.44
  1.6 2.8 %collective-permute-start.1 = (f32[1,32,128]{2,1,0:T(8,128)}, f32[1,32,128]{2,1,0:T(8,128)S(1)}, u32[]{:S(2)}, u32[]{:S(2)}) collective-permute-start(f32[1,32,128]{2,1,0:T(8,128)} %get-tuple-element.69), channel_id=1, source_target_pairs={{1,0},{2,1},{3,2},{4,3},{5,4},{6,5},{7,6},{8,7},{9,8},{10,9},{11,1... | collective-permute-start | bytes 49160 | tf_op jit(solution)/shard_map/ppermute | solution.py:13
  4.4 4.1 %collective-permute-start = (f32[1,32,128]{2,1,0:T(8,128)}, f32[1,32,128]{2,1,0:T(8,128)S(1)}, u32[]{:S(2)}, u32[]{:S(2)}) collective-permute-start(f32[1,32,128]{2,1,0:T(8,128)} %get-tuple-element.70), channel_id=1, source_target_pairs={{0,1},{1,2},{2,3},{3,4},{4,5},{5,6},{6,7},{7,8},{8,9},{9,10},{10,1... | collective-permute-start | bytes 49160 | tf_op jit(solution)/shard_map/ppermute | solution.py:13
  8.6 1.6 %fusion.2 = f32[2,32,512]{2,1,0:T(8,128)S(1)} fusion(bf16[4,512,512]{2,1,0:T(8,128)(2,1)} %param.15, f32[2,32,512]{2,1,0:T(8,128)S(1)} %fusion.12), kind=kOutput, calls=%fused_computation.7 | convolution fusion | flops 33587200 | bytes 1310720 | tf_op jit(solution)/shard_map/srk,sjk->srj/dot_general | solution.py:49
  10.3 0.3 fusion.17
  10.7 0.6 pad.14.clone
  11.4 0.2 convolution_bitcast_fusion.3
  11.7 0.4 fusion.4
  12.2 14.7 %all-gather = f32[352,128]{1,0:T(8,128)S(1)} all-gather(f32[88,128]{1,0:T(8,128)S(1)} %get-tuple-element.78), channel_id=2, replica_groups=mesh['x'=4,'z'=16,'core'=2,'sub'=4] {'sub'}, dimensions={0}, use_global_device_ids=true | all-gather | bytes 225280 | tf_op jit(solution)/shard_map/all_gather | solution.py:67
  27.0 0.2 convolution_bitcast_fusion.2
  27.2 0.2 convolution_bitcast_fusion.1
  27.5 1.8 %all_gather.17 = f32[64,32]{1,0:T(8,128)S(1)} all-gather(f32[32,32]{1,0:T(8,128)S(1)} %copy.18), channel_id=1, replica_groups=mesh['x'=4,'z'=16,'core'=2,'sub'=4] {'core'}, dimensions={0}, use_global_device_ids=true | all-gather | bytes 12288 | tf_op jit(solution)/shard_map/all_gather | solution.py:91
  29.4 3.8 %collective-permute-start.2 = (f32[304,128]{1,0:T(8,128)S(1)}, f32[304,128]{1,0:T(8,128)S(1)}, u32[]{:S(2)}, u32[]{:S(2)}) collective-permute-start(f32[304,128]{1,0:T(8,128)S(1)} %select_maximum_fusion), channel_id=1, source_target_pairs={{3,4},{7,8},{11,12},{15,16},{19,20},{23,24},{27,28},{31,32},{35,36... | collective-permute-start | bytes 466952 | tf_op jit(solution)/shard_map/ppermute | solution.py:87
  33.2 35.2 %all-gather.1 = f32[16,64,32]{1,2,0:T(8,128)S(1)} all-gather(f32[1,64,32]{1,2,0:T(8,128)S(1)} %copy.19), channel_id=1, replica_groups=mesh['x'=4,'z'=16,'core'=2,'sub'=4] {'z'}, dimensions={0}, use_global_device_ids=true | all-gather | bytes 139264 | tf_op jit(solution)/shard_map/all_gather | solution.py:91
  68.3 0.2 copy.20
  68.7 14.0 %all_gather.19 = f32[4096,32]{0,1:T(8,128)S(1)} all-gather(f32[1024,32]{0,1:T(8,128)S(1)} %reshape.144), channel_id=1, replica_groups=mesh['x'=4,'z'=16,'core'=2,'sub'=4] {'x'}, dimensions={0}, use_global_device_ids=true | all-gather | bytes 655360 | tf_op jit(solution)/shard_map/all_gather | solution.py:91
  82.7 0.4 fusion.47
  83.1 0.2 fusion.1
  83.3 0.2 fusion.21
  83.6 0.2 fusion.19
  83.9 0.3 select_bitcast_fusion.1
  84.3 0.1 multiply_reduce_fusion
  84.5 1.0 %fusion = f32[4,32,512]{2,1,0:T(8,128)} fusion(f32[4,8,512]{2,1,0:T(8,128)S(1)} %copy-done.2, f32[4,32,128]{2,1,0:T(8,128)S(1)} %get-tuple-element.82, f32[4,32,128]{2,1,0:T(8,128)S(1)} %get-tuple-element.81, f32[512]{0:T(512)S(1)} %copy-done.5, f32[128,32]{1,0:T(8,128)S(1)} %fusion.1, s32[]{:T(128)S(6)} %select_n.84, ...), kind=kOutput, calls=%fused_computation.1 | convolution fusion | flops 3538944 | bytes 739332 | tf_op jit(solution)/shard_map/snk,snr->srk/dot_general | solution.py:129
  (51 shorter events, 0.8 us)
Async XLA Ops:
  0.0 10.2 %copy-start = (f32[32,4096]{1,0:T(8,128)S(1)}, f32[32,4096]{1,0:T(8,128)}, u32[]{:S(2)}) copy-start(f32[32,4096]{1,0:T(8,128)} %param.19) | copy-start | bytes 1572868
  0.0 11.4 %copy-start.2 = (f32[4,8,512]{2,1,0:T(8,128)S(1)}, f32[4,8,512]{2,1,0:T(8,128)}, u32[]{:S(2)}) copy-start(f32[4,8,512]{2,1,0:T(8,128)} %param.16) | copy-start | bytes 196612
  0.0 10.3 %copy-start.3 = (f32[1,32,128]{2,1,0:T(8,128)S(1)}, f32[1,32,128]{2,1,0:T(8,128)}, u32[]{:S(2)}) copy-start(f32[1,32,128]{2,1,0:T(8,128)} %param.18) | copy-start | bytes 49156
  1.0 10.7 %copy-start.1 = (bf16[4,512,512]{2,1,0:T(8,128)(2,1)S(1)}, bf16[4,512,512]{2,1,0:T(8,128)(2,1)}, u32[]{:S(2)}) copy-start(bf16[4,512,512]{2,1,0:T(8,128)(2,1)} %param.15) | copy-start | bytes 6291460
  1.6 9.7 %collective-permute-start.1 = (f32[1,32,128]{2,1,0:T(8,128)}, f32[1,32,128]{2,1,0:T(8,128)S(1)}, u32[]{:S(2)}, u32[]{:S(2)}) collective-permute-start(f32[1,32,128]{2,1,0:T(8,128)} %get-tuple-element.69), channel_id=1, source_target_pairs={{1,0},{2,1},{3,2},{4,3},{5,4},{6,5},{7,6},{8,7},{9,8},{10,9},{11,1... | collective-permute-start | bytes 49160 | tf_op jit(solution)/shard_map/ppermute | solution.py:13
  4.4 6.9 %collective-permute-start = (f32[1,32,128]{2,1,0:T(8,128)}, f32[1,32,128]{2,1,0:T(8,128)S(1)}, u32[]{:S(2)}, u32[]{:S(2)}) collective-permute-start(f32[1,32,128]{2,1,0:T(8,128)} %get-tuple-element.70), channel_id=1, source_target_pairs={{0,1},{1,2},{2,3},{3,4},{4,5},{5,6},{6,7},{7,8},{8,9},{9,10},{10,1... | collective-permute-start | bytes 49160 | tf_op jit(solution)/shard_map/ppermute | solution.py:13
  10.3 16.9 %copy-start.4 = (f32[1,128,128]{2,1,0:T(8,128)S(1)}, f32[1,128,128]{2,1,0:T(8,128)}, u32[]{:S(2)}) copy-start(f32[1,128,128]{2,1,0:T(8,128)} %param.17) | copy-start | bytes 196612
  29.4 53.3 %collective-permute-start.2 = (f32[304,128]{1,0:T(8,128)S(1)}, f32[304,128]{1,0:T(8,128)S(1)}, u32[]{:S(2)}, u32[]{:S(2)}) collective-permute-start(f32[304,128]{1,0:T(8,128)S(1)} %select_maximum_fusion), channel_id=1, source_target_pairs={{3,4},{7,8},{11,12},{15,16},{19,20},{23,24},{27,28},{31,32},{35,36... | collective-permute-start | bytes 466952 | tf_op jit(solution)/shard_map/ppermute | solution.py:87
  68.7 15.8 %copy-start.5 = (f32[512]{0:T(512)S(1)}, f32[512]{0:T(512)}, u32[]{:S(2)}) copy-start(f32[512]{0:T(512)} %pad.14.clone) | copy-start | bytes 6148

commit v9 on v7

--- a/solution.py
+++ b/solution.py
@@ -118,7 +118,11 @@
     rims = rim_local + jnp.sum(rim_basis[:, :, None, :] * rim_coef[:, :, :, None], axis=1)
     from_before = rims[0:1]
     from_behind = rims[1:2]
-    return add_rims(update, from_before, from_behind)
+    lower_rim = update[:, :, :IFW]
+    upper_rim = update[:, :, nloc - IFW :]
+    new_lower = lower_rim + 0.5 * jnp.concatenate([from_before, upper_rim[:-1]], 0)
+    new_upper = upper_rim + 0.5 * jnp.concatenate([lower_rim[1:], from_behind], 0)
+    return jnp.concatenate([new_lower, update[:, :, IFW : nloc - IFW], new_upper], 2)
 
 
 def solution(mesh):

time: 84.9 us -> 83.5 us (0.984)
    scatter-add x2 -> x1, other arithmetic: 1.49 us -> 0.02 us  [add_rims(): return coupled.at[:, :, values_in.shape[2] - IFW:].add(0.5 * next_rims)]
    unnamed x17 -> x15, local copies, waits for them, and re-layouts: 2.03 us -> 1.34 us
where the time goes in v9:
time: 83.5 us; the launch traced here: 83.2 us
  blocking collectives  67 us (80%)
  starting transfers between devices  7.75 us (9%)
  matrix products  4.3 us (5%)
  local copies, waits for them, and re-layouts  2.46 us (3%)
  other arithmetic  1.03 us (1%)
    all_gather x3, blocking collectives, shards(): gathered_in = lax.all_gather(gathered_in, axis, axis=0, tiled=True)  53.3 us
    all_gather x1, blocking collectives, shards(): gathered = lax.all_gather(packed, 'sub', axis=0, tiled=False)  13.6 us
    ppermute x2, starting transfers between devices, from_behind_2(): return lax.ppermute(array, axis, pairs)  5.83 us
    ppermute x1, starting transfers between devices, shards(): incoming = lax.ppermute(outgoing, SPREAD, pairs)  1.92 us
  transfers between devices with their start and end apart: 3, of which 1 were waited for; matrix products, arithmetic and copies ran while one was open for 4% of the time, Pallas kernels for 0%

profile of v9, /device:TPU:24, one launch (start us, length us, event | category | flops | bytes accessed | tf_op | source)
XLA Modules:
  0.0 83.2 jit_solution(1764405446021717086)
XLA Ops:
  0.0 1.1 %copy.33 = f32[4,32,512]{2,1,0:T(8,128)S(1)} copy(f32[4,32,512]{2,1,0:T(8,128)} %param.14) | data formatting | bytes 524288
  1.1 0.6 fusion.33
  1.7 1.9 %collective-permute-start = (f32[1,32,128]{2,1,0:T(8,128)}, f32[1,32,128]{2,1,0:T(8,128)S(1)}, u32[]{:S(2)}, u32[]{:S(2)}) collective-permute-start(f32[1,32,128]{2,1,0:T(8,128)} %get-tuple-element.64), channel_id=1, source_target_pairs={{0,1},{1,2},{2,3},{3,4},{4,5},{5,6},{6,7},{7,8},{8,9},{9,10},{10,1... | collective-permute-start | bytes 49160 | tf_op jit(solution)/shard_map/ppermute | solution.py:13
  3.6 3.9 %collective-permute-start.1 = (f32[1,32,128]{2,1,0:T(8,128)}, f32[1,32,128]{2,1,0:T(8,128)S(1)}, u32[]{:S(2)}, u32[]{:S(2)}) collective-permute-start(f32[1,32,128]{2,1,0:T(8,128)} %get-tuple-element.63), channel_id=1, source_target_pairs={{1,0},{2,1},{3,2},{4,3},{5,4},{6,5},{7,6},{8,7},{9,8},{10,9},{11,1... | collective-permute-start | bytes 49160 | tf_op jit(solution)/shard_map/ppermute | solution.py:13
  7.7 1.7 %fusion.1 = f32[2,32,512]{2,1,0:T(8,128)S(1)} fusion(bf16[4,512,512]{2,1,0:T(8,128)(2,1)} %param.15, f32[2,32,512]{2,1,0:T(8,128)S(1)} %fusion.11), kind=kOutput, calls=%fused_computation.6 | convolution fusion | flops 33587200 | bytes 1310720 | tf_op jit(solution)/shard_map/srk,sjk->srj/dot_general | solution.py:49
  9.3 0.3 fusion.16
  9.8 0.3 collective-permute-done.1
  10.2 0.4 fusion.3
  10.6 0.2 convolution_bitcast_fusion.3
  11.0 13.6 %all-gather = f32[352,128]{1,0:T(8,128)S(1)} all-gather(f32[88,128]{1,0:T(8,128)S(1)} %constant_dynamic-update-slice_fusion), channel_id=2, replica_groups=mesh['x'=4,'z'=16,'core'=2,'sub'=4] {'sub'}, dimensions={0}, use_global_device_ids=true | all-gather | bytes 225280 | tf_op jit(solution)/shard_map/all_gather | solution.py:67
  24.7 0.2 convolution_bitcast_fusion.2
  24.9 0.2 convolution_bitcast_fusion.1
  25.1 1.9 %collective-permute-start.2 = (f32[304,128]{1,0:T(8,128)S(1)}, f32[304,128]{1,0:T(8,128)S(1)}, u32[]{:S(2)}, u32[]{:S(2)}) collective-permute-start(f32[304,128]{1,0:T(8,128)S(1)} %select_maximum_fusion), channel_id=1, source_target_pairs={{3,4},{7,8},{11,12},{15,16},{19,20},{23,24},{27,28},{31,32},{35,36... | collective-permute-start | bytes 466952 | tf_op jit(solution)/shard_map/ppermute | solution.py:86
  27.1 3.3 %all_gather.17 = f32[64,32]{1,0:T(8,128)S(1)} all-gather(f32[32,32]{1,0:T(8,128)S(1)} %copy.18), channel_id=1, replica_groups=mesh['x'=4,'z'=16,'core'=2,'sub'=4] {'core'}, dimensions={0}, use_global_device_ids=true | all-gather | bytes 12288 | tf_op jit(solution)/shard_map/all_gather | solution.py:90
  30.5 37.0 %all-gather.1 = f32[16,64,32]{1,2,0:T(8,128)S(1)} all-gather(f32[1,64,32]{1,2,0:T(8,128)S(1)} %copy.19), channel_id=1, replica_groups=mesh['x'=4,'z'=16,'core'=2,'sub'=4] {'z'}, dimensions={0}, use_global_device_ids=true | all-gather | bytes 139264 | tf_op jit(solution)/shard_map/all_gather | solution.py:90
  67.4 0.2 copy.20
  67.6 0.1 reshape.144
  67.7 13.1 %all_gather.19 = f32[4096,32]{0,1:T(8,128)S(1)} all-gather(f32[1024,32]{0,1:T(8,128)S(1)} %reshape.144), channel_id=1, replica_groups=mesh['x'=4,'z'=16,'core'=2,'sub'=4] {'x'}, dimensions={0}, use_global_device_ids=true | all-gather | bytes 655360 | tf_op jit(solution)/shard_map/all_gather | solution.py:90
  80.8 0.4 fusion.36
  81.2 0.2 fusion
  81.5 0.3 convolution_add_fusion
  81.9 0.3 select_bitcast_fusion.1
  82.3 0.1 multiply_reduce_fusion
  82.5 0.7 pad_maximum_fusion
  (44 shorter events, 0.6 us)
Async XLA Ops:
  0.0 9.3 %copy-start = (f32[32,4096]{1,0:T(8,128)S(1)}, f32[32,4096]{1,0:T(8,128)}, u32[]{:S(2)}) copy-start(f32[32,4096]{1,0:T(8,128)} %param.19) | copy-start | bytes 1572868
  0.0 10.2 %copy-start.1 = (bf16[4,512,512]{2,1,0:T(8,128)(2,1)S(1)}, bf16[4,512,512]{2,1,0:T(8,128)(2,1)}, u32[]{:S(2)}) copy-start(bf16[4,512,512]{2,1,0:T(8,128)(2,1)} %param.15) | copy-start | bytes 6291460
  0.0 9.3 %copy-start.3 = (f32[1,32,128]{2,1,0:T(8,128)S(1)}, f32[1,32,128]{2,1,0:T(8,128)}, u32[]{:S(2)}) copy-start(f32[1,32,128]{2,1,0:T(8,128)} %param.18) | copy-start | bytes 49156
  1.7 8.1 %collective-permute-start = (f32[1,32,128]{2,1,0:T(8,128)}, f32[1,32,128]{2,1,0:T(8,128)S(1)}, u32[]{:S(2)}, u32[]{:S(2)}) collective-permute-start(f32[1,32,128]{2,1,0:T(8,128)} %get-tuple-element.64), channel_id=1, source_target_pairs={{0,1},{1,2},{2,3},{3,4},{4,5},{5,6},{6,7},{7,8},{8,9},{9,10},{10,1... | collective-permute-start | bytes 49160 | tf_op jit(solution)/shard_map/ppermute | solution.py:13
  3.6 6.5 %collective-permute-start.1 = (f32[1,32,128]{2,1,0:T(8,128)}, f32[1,32,128]{2,1,0:T(8,128)S(1)}, u32[]{:S(2)}, u32[]{:S(2)}) collective-permute-start(f32[1,32,128]{2,1,0:T(8,128)} %get-tuple-element.63), channel_id=1, source_target_pairs={{1,0},{2,1},{3,2},{4,3},{5,4},{6,5},{7,6},{8,7},{9,8},{10,9},{11,1... | collective-permute-start | bytes 49160 | tf_op jit(solution)/shard_map/ppermute | solution.py:13
  7.6 2.9 %copy-start.2 = (f32[4,8,512]{2,1,0:T(8,128)S(1)}, f32[4,8,512]{2,1,0:T(8,128)}, u32[]{:S(2)}) copy-start(f32[4,8,512]{2,1,0:T(8,128)} %param.16) | copy-start | bytes 196612
  9.3 15.6 %copy-start.4 = (f32[1,128,128]{2,1,0:T(8,128)S(1)}, f32[1,128,128]{2,1,0:T(8,128)}, u32[]{:S(2)}) copy-start(f32[1,128,128]{2,1,0:T(8,128)} %param.17) | copy-start | bytes 196612
  25.1 56.7 %collective-permute-start.2 = (f32[304,128]{1,0:T(8,128)S(1)}, f32[304,128]{1,0:T(8,128)S(1)}, u32[]{:S(2)}, u32[]{:S(2)}) collective-permute-start(f32[304,128]{1,0:T(8,128)S(1)} %select_maximum_fusion), channel_id=1, source_target_pairs={{3,4},{7,8},{11,12},{15,16},{19,20},{23,24},{27,28},{31,32},{35,36... | collective-permute-start | bytes 466952 | tf_op jit(solution)/shard_map/ppermute | solution.py:86

commit v10 on v9

--- a/solution.py
+++ b/solution.py
@@ -83,11 +83,12 @@
         [fold.reshape(fold_rows, IFW), edge_local, edge_basis, jnp.pad(edge_rows, ((0, 0), (0, IFW - nrhs)))], 0)
     count = lax.axis_size(SPREAD)
     pairs = [(i, i + 1) for i in range(sub - 1, count - 1, sub)] + [(i + 1, i) for i in range(sub - 1, count - 1, sub)]
+    gathered_in = level3_in
+    for axis in ("core", "z"):
+        gathered_in = lax.all_gather(gathered_in, axis, axis=0, tiled=True)
+    outgoing, gathered_in = lax.optimization_barrier((outgoing, gathered_in))
     incoming = lax.ppermute(outgoing, SPREAD, pairs)
-
-    gathered_in = level3_in
-    for axis in ("core", "z", "x"):
-        gathered_in = lax.all_gather(gathered_in, axis, axis=0, tiled=True)
+    gathered_in = lax.all_gather(gathered_in, "x", axis=0, tiled=True)
     level3 = jnp.dot(level3_inverse, gathered_in, precision=high)
     corrected = level2 + jnp.dot(level2_basis[0].T, level3, precision=high)
     own_count = coarse.shape[0] * coarse.shape[1]

time: 83.5 us -> 83.1 us (level)
  the two profiles are of different devices: /device:TPU:24 before, /device:TPU:1 now
where the time goes in v10:
time: 83.1 us; the launch traced here: 82.9 us
  blocking collectives  56 us (67%)
  starting transfers between devices  18.6 us (22%)
  matrix products  4.3 us (5%)
  local copies, waits for them, and re-layouts  2.46 us (3%)
  other arithmetic  1.03 us (1%)
    all_gather x2, blocking collectives, shards(): gathered_in = lax.all_gather(gathered_in, axis, axis=0, tiled=True)  33.2 us
    all_gather x1, blocking collectives, shards(): gathered_in = lax.all_gather(gathered_in, 'x', axis=0, tiled=True)  11.7 us
    all_gather x1, blocking collectives, shards(): gathered = lax.all_gather(packed, 'sub', axis=0, tiled=False)  11.1 us
    ppermute x1, starting transfers between devices, shards(): incoming = lax.ppermute(outgoing, SPREAD, pairs)  10.7 us
    ppermute x2, starting transfers between devices, from_behind_2(): return lax.ppermute(array, axis, pairs)  7.94 us
  transfers between devices with their start and end apart: 3, of which 0 were waited for; matrix products, arithmetic and copies ran while one was open for 4% of the time, Pallas kernels for 0%

profile of v10, /device:TPU:1, one launch (start us, length us, event | category | flops | bytes accessed | tf_op | source)
XLA Modules:
  0.0 82.9 jit_solution(5125979693414574033)
XLA Ops:
  0.0 1.1 %copy.33 = f32[4,32,512]{2,1,0:T(8,128)S(1)} copy(f32[4,32,512]{2,1,0:T(8,128)} %param.14) | data formatting | bytes 524288
  1.1 0.6 fusion.33
  1.7 4.0 %collective-permute-start = (f32[1,32,128]{2,1,0:T(8,128)}, f32[1,32,128]{2,1,0:T(8,128)S(1)}, u32[]{:S(2)}, u32[]{:S(2)}) collective-permute-start(f32[1,32,128]{2,1,0:T(8,128)} %get-tuple-element.68), channel_id=1, source_target_pairs={{0,1},{1,2},{2,3},{3,4},{4,5},{5,6},{6,7},{7,8},{8,9},{9,10},{10,1... | collective-permute-start | bytes 49160 | tf_op jit(solution)/shard_map/ppermute | solution.py:13
  5.8 3.9 %collective-permute-start.1 = (f32[1,32,128]{2,1,0:T(8,128)}, f32[1,32,128]{2,1,0:T(8,128)S(1)}, u32[]{:S(2)}, u32[]{:S(2)}) collective-permute-start(f32[1,32,128]{2,1,0:T(8,128)} %get-tuple-element.67), channel_id=1, source_target_pairs={{1,0},{2,1},{3,2},{4,3},{5,4},{6,5},{7,6},{8,7},{9,8},{10,9},{11,1... | collective-permute-start | bytes 49160 | tf_op jit(solution)/shard_map/ppermute | solution.py:13
  9.8 1.7 %fusion.1 = f32[2,32,512]{2,1,0:T(8,128)S(1)} fusion(bf16[4,512,512]{2,1,0:T(8,128)(2,1)} %param.15, f32[2,32,512]{2,1,0:T(8,128)S(1)} %fusion.11), kind=kOutput, calls=%fused_computation.6 | convolution fusion | flops 33587200 | bytes 1310720 | tf_op jit(solution)/shard_map/srk,sjk->srj/dot_general | solution.py:49
  11.5 0.3 fusion.16
  12.0 0.4 fusion.3
  12.4 0.2 convolution_bitcast_fusion.3
  12.8 11.1 %all-gather = f32[352,128]{1,0:T(8,128)S(1)} all-gather(f32[88,128]{1,0:T(8,128)S(1)} %constant_dynamic-update-slice_fusion), channel_id=2, replica_groups=mesh['x'=4,'z'=16,'core'=2,'sub'=4] {'sub'}, dimensions={0}, use_global_device_ids=true | all-gather | bytes 225280 | tf_op jit(solution)/shard_map/all_gather | solution.py:67
  23.9 0.1 reshape.138
  24.0 0.2 convolution_bitcast_fusion.2
  24.2 0.2 convolution_bitcast_fusion.1
  24.5 6.2 %all_gather.17 = f32[64,32]{1,0:T(8,128)S(1)} all-gather(f32[32,32]{1,0:T(8,128)S(1)} %copy.18), channel_id=1, replica_groups=mesh['x'=4,'z'=16,'core'=2,'sub'=4] {'core'}, dimensions={0}, use_global_device_ids=true | all-gather | bytes 12288 | tf_op jit(solution)/shard_map/all_gather | solution.py:88
  30.8 27.0 %all-gather.1 = f32[16,64,32]{1,2,0:T(8,128)S(1)} all-gather(f32[1,64,32]{1,2,0:T(8,128)S(1)} %copy.19), channel_id=1, replica_groups=mesh['x'=4,'z'=16,'core'=2,'sub'=4] {'z'}, dimensions={0}, use_global_device_ids=true | all-gather | bytes 139264 | tf_op jit(solution)/shard_map/all_gather | solution.py:88
  57.8 0.2 copy.20
  58.0 0.1 reshape.144
  58.1 10.7 %collective-permute-start.2 = (f32[304,128]{1,0:T(8,128)S(1)}, f32[304,128]{1,0:T(8,128)S(1)}, u32[]{:S(2)}, u32[]{:S(2)}) collective-permute-start(f32[304,128]{1,0:T(8,128)S(1)} %select_maximum_fusion), channel_id=1, source_target_pairs={{3,4},{7,8},{11,12},{15,16},{19,20},{23,24},{27,28},{31,32},{35,36... | collective-permute-start | bytes 466952 | tf_op jit(solution)/shard_map/ppermute | solution.py:90
  68.8 11.7 %all_gather.19 = f32[4096,32]{0,1:T(8,128)S(1)} all-gather(f32[1024,32]{0,1:T(8,128)S(1)} %reshape.144), channel_id=1, replica_groups=mesh['x'=4,'z'=16,'core'=2,'sub'=4] {'x'}, dimensions={0}, use_global_device_ids=true | all-gather | bytes 655360 | tf_op jit(solution)/shard_map/all_gather | solution.py:91
  80.5 0.4 fusion.36
  80.8 0.2 fusion
  81.1 0.3 convolution_add_fusion
  81.6 0.3 select_bitcast_fusion.1
  81.9 0.1 multiply_reduce_fusion
  82.1 0.7 pad_maximum_fusion
  (44 shorter events, 0.6 us)
Async XLA Ops:
  0.0 11.4 %copy-start = (f32[32,4096]{1,0:T(8,128)S(1)}, f32[32,4096]{1,0:T(8,128)}, u32[]{:S(2)}) copy-start(f32[32,4096]{1,0:T(8,128)} %param.19) | copy-start | bytes 1572868
  0.0 12.0 %copy-start.1 = (bf16[4,512,512]{2,1,0:T(8,128)(2,1)S(1)}, bf16[4,512,512]{2,1,0:T(8,128)(2,1)}, u32[]{:S(2)}) copy-start(bf16[4,512,512]{2,1,0:T(8,128)(2,1)} %param.15) | copy-start | bytes 6291460
  0.0 11.4 %copy-start.3 = (f32[1,32,128]{2,1,0:T(8,128)S(1)}, f32[1,32,128]{2,1,0:T(8,128)}, u32[]{:S(2)}) copy-start(f32[1,32,128]{2,1,0:T(8,128)} %param.18) | copy-start | bytes 49156
  1.7 10.2 %collective-permute-start = (f32[1,32,128]{2,1,0:T(8,128)}, f32[1,32,128]{2,1,0:T(8,128)S(1)}, u32[]{:S(2)}, u32[]{:S(2)}) collective-permute-start(f32[1,32,128]{2,1,0:T(8,128)} %get-tuple-element.68), channel_id=1, source_target_pairs={{0,1},{1,2},{2,3},{3,4},{4,5},{5,6},{6,7},{7,8},{8,9},{9,10},{10,1... | collective-permute-start | bytes 49160 | tf_op jit(solution)/shard_map/ppermute | solution.py:13
  5.8 6.2 %collective-permute-start.1 = (f32[1,32,128]{2,1,0:T(8,128)}, f32[1,32,128]{2,1,0:T(8,128)S(1)}, u32[]{:S(2)}, u32[]{:S(2)}) collective-permute-start(f32[1,32,128]{2,1,0:T(8,128)} %get-tuple-element.67), channel_id=1, source_target_pairs={{1,0},{2,1},{3,2},{4,3},{5,4},{6,5},{7,6},{8,7},{9,8},{10,9},{11,1... | collective-permute-start | bytes 49160 | tf_op jit(solution)/shard_map/ppermute | solution.py:13
  9.8 2.7 %copy-start.2 = (f32[4,8,512]{2,1,0:T(8,128)S(1)}, f32[4,8,512]{2,1,0:T(8,128)}, u32[]{:S(2)}) copy-start(f32[4,8,512]{2,1,0:T(8,128)} %param.16) | copy-start | bytes 196612
  11.4 12.8 %copy-start.4 = (f32[1,128,128]{2,1,0:T(8,128)S(1)}, f32[1,128,128]{2,1,0:T(8,128)}, u32[]{:S(2)}) copy-start(f32[1,128,128]{2,1,0:T(8,128)} %param.17) | copy-start | bytes 196612
  58.1 23.4 %collective-permute-start.2 = (f32[304,128]{1,0:T(8,128)S(1)}, f32[304,128]{1,0:T(8,128)S(1)}, u32[]{:S(2)}, u32[]{:S(2)}) collective-permute-start(f32[304,128]{1,0:T(8,128)S(1)} %select_maximum_fusion), channel_id=1, source_target_pairs={{3,4},{7,8},{11,12},{15,16},{19,20},{23,24},{27,28},{31,32},{35,36... | collective-permute-start | bytes 466952 | tf_op jit(solution)/shard_map/ppermute | solution.py:90

commit v11 on v10

--- a/solution.py
+++ b/solution.py
@@ -83,12 +83,12 @@
         [fold.reshape(fold_rows, IFW), edge_local, edge_basis, jnp.pad(edge_rows, ((0, 0), (0, IFW - nrhs)))], 0)
     count = lax.axis_size(SPREAD)
     pairs = [(i, i + 1) for i in range(sub - 1, count - 1, sub)] + [(i + 1, i) for i in range(sub - 1, count - 1, sub)]
-    gathered_in = level3_in
+    gathered_in = level3_in.reshape(-1, IFW)
     for axis in ("core", "z"):
         gathered_in = lax.all_gather(gathered_in, axis, axis=0, tiled=True)
     outgoing, gathered_in = lax.optimization_barrier((outgoing, gathered_in))
     incoming = lax.ppermute(outgoing, SPREAD, pairs)
-    gathered_in = lax.all_gather(gathered_in, "x", axis=0, tiled=True)
+    gathered_in = lax.all_gather(gathered_in, "x", axis=0, tiled=True).reshape(-1, nrhs)
     level3 = jnp.dot(level3_inverse, gathered_in, precision=high)
     corrected = level2 + jnp.dot(level2_basis[0].T, level3, precision=high)
     own_count = coarse.shape[0] * coarse.shape[1]

time: 83.1 us -> 92.4 us (1.11)
  the two profiles are of different devices: /device:TPU:1 before, /device:TPU:25 now
where the time goes in v11:
time: 92.4 us; the launch traced here: 91.9 us
  blocking collectives  56.4 us (61%)
  starting transfers between devices  20.4 us (22%)
  matrix products  7.53 us (8%)
  local copies, waits for them, and re-layouts  4.15 us (4%)
  other arithmetic  3.09 us (3%)
    all_gather x2, blocking collectives, shards(): gathered_in = lax.all_gather(gathered_in, axis, axis=0, tiled=True)  33.2 us
    all_gather x1, blocking collectives, shards(): lax.all_gather(gathered_in, 'x', axis=0, tiled=True).reshape(-1, nrhs)  14.1 us
    ppermute x1, starting transfers between devices, shards(): incoming = lax.ppermute(outgoing, SPREAD, pairs)  12.6 us
    all_gather x1, blocking collectives, shards(): gathered = lax.all_gather(packed, 'sub', axis=0, tiled=False)  9.2 us
    ppermute x2, starting transfers between devices, from_behind_2(): return lax.ppermute(array, axis, pairs)  7.79 us
  transfers between devices with their start and end apart: 3, of which 0 were waited for; matrix products, arithmetic and copies ran while one was open for 6% of the time, Pallas kernels for 0%

profile of v11, /device:TPU:25, one launch (start us, length us, event | category | flops | bytes accessed | tf_op | source)
XLA Modules:
  0.0 91.9 jit_solution(11476867220264260999)
XLA Ops:
  0.0 1.0 %copy.26 = f32[4,32,512]{2,1,0:T(8,128)S(1)} copy(f32[4,32,512]{2,1,0:T(8,128)} %param.14) | data formatting | bytes 524288
  1.0 2.5 %collective-permute-start.1 = (f32[1,32,128]{2,1,0:T(8,128)S(1)}, f32[1,32,128]{2,1,0:T(8,128)S(1)}, u32[]{:S(2)}, u32[]{:S(2)}) collective-permute-start(f32[1,32,128]{2,1,0:T(8,128)S(1)} %get-tuple-element.67), channel_id=1, source_target_pairs={{1,0},{2,1},{3,2},{4,3},{5,4},{6,5},{7,6},{8,7},{9,8},{10,9},{11,1... | collective-permute-start | bytes 49160 | tf_op jit(solution)/shard_map/ppermute | solution.py:13
  3.5 5.3 %collective-permute-start = (f32[1,32,128]{2,1,0:T(8,128)S(1)}, f32[1,32,128]{2,1,0:T(8,128)S(1)}, u32[]{:S(2)}, u32[]{:S(2)}) collective-permute-start(f32[1,32,128]{2,1,0:T(8,128)S(1)} %get-tuple-element.68), channel_id=1, source_target_pairs={{0,1},{1,2},{2,3},{3,4},{4,5},{5,6},{6,7},{7,8},{8,9},{9,10},{10,1... | collective-permute-start | bytes 49160 | tf_op jit(solution)/shard_map/ppermute | solution.py:13
  8.9 1.6 %fusion.1 = f32[2,32,512]{2,1,0:T(8,128)S(1)} fusion(bf16[4,512,512]{2,1,0:T(8,128)(2,1)} %param.15, f32[2,32,512]{2,1,0:T(8,128)S(1)} %fusion.11), kind=kOutput, calls=%fused_computation.6 | convolution fusion | flops 33587200 | bytes 1310720 | tf_op jit(solution)/shard_map/srk,sjk->srj/dot_general | solution.py:49
  10.6 0.3 fusion.16
  11.4 0.4 fusion.3
  11.8 0.7 fusion.34
  12.5 9.2 %all-gather = f32[352,128]{1,0:T(8,128)S(1)} all-gather(f32[88,128]{1,0:T(8,128)S(1)} %constant_dynamic-update-slice_fusion), channel_id=2, replica_groups=mesh['x'=4,'z'=16,'core'=2,'sub'=4] {'sub'}, dimensions={0}, use_global_device_ids=true | all-gather | bytes 225280 | tf_op jit(solution)/shard_map/all_gather | solution.py:67
  22.0 1.0 %convolution_bitcast_fusion.1 = f32[128,32]{1,0:T(8,128)S(1)} fusion(f32[128,32]{1,0:T(8,128)S(1)} %reshape.144, f32[1,128,128]{2,1,0:T(8,128)} %param.17), kind=kOutput, calls=%fused_computation.3 | convolution fusion | flops 3145728 | bytes 98304 | tf_op jit(solution)/shard_map/dot_general | solution.py:69
  23.2 7.1 %all_gather.17 = f32[16,128]{1,0:T(8,128)S(1)} all-gather(f32[8,128]{1,0:T(8,128)S(1)} %reshape.146), channel_id=1, replica_groups=mesh['x'=4,'z'=16,'core'=2,'sub'=4] {'core'}, dimensions={0}, use_global_device_ids=true | all-gather | bytes 12288 | tf_op jit(solution)/shard_map/all_gather | solution.py:88
  30.4 26.0 %all_gather.18 = f32[256,128]{1,0:T(8,128)S(1)} all-gather(f32[16,128]{1,0:T(8,128)S(1)} %all_gather.17), channel_id=1, replica_groups=mesh['x'=4,'z'=16,'core'=2,'sub'=4] {'z'}, dimensions={0}, use_global_device_ids=true | all-gather | bytes 139264 | tf_op jit(solution)/shard_map/all_gather | solution.py:88
  56.4 0.7 select_maximum_fusion
  57.1 12.6 %collective-permute-start.2 = (f32[304,128]{1,0:T(8,128)}, f32[304,128]{1,0:T(8,128)}, u32[]{:S(2)}, u32[]{:S(2)}) collective-permute-start(f32[304,128]{1,0:T(8,128)} %select_maximum_fusion), channel_id=1, source_target_pairs={{3,4},{7,8},{11,12},{15,16},{19,20},{23,24},{27,28},{31,32},{35,36... | collective-permute-start | bytes 466952 | tf_op jit(solution)/shard_map/ppermute | solution.py:90
  69.6 14.1 %all_gather.19 = f32[1024,128]{1,0:T(8,128)S(1)} all-gather(f32[256,128]{1,0:T(8,128)S(1)} %all_gather.18), channel_id=1, replica_groups=mesh['x'=4,'z'=16,'core'=2,'sub'=4] {'x'}, dimensions={0}, use_global_device_ids=true | all-gather | bytes 655360 | tf_op jit(solution)/shard_map/all_gather | solution.py:91
  83.7 0.5 reshape.147
  84.2 1.8 %fusion.36 = f32[32,32]{1,0:T(8,128)S(1)} fusion(f32[4096,32]{1,0:T(8,128)S(1)} %reshape.147, f32[32,4096]{1,0:T(8,128)S(1)} %copy-done), kind=kOutput, calls=%fused_computation.72 | convolution fusion | flops 25165824 | bytes 1052672 | tf_op jit(solution)/shard_map/dot_general | solution.py:92
  86.0 0.3 fusion
  86.3 0.3 convolution_add_fusion
  86.6 0.6 fusion.31
  87.3 0.9 slice.288
  88.2 0.7 fusion.27
  88.9 1.3 %select_bitcast_fusion.1 = (f32[1,8,32]{2,1,0:T(8,128)S(1)}, f32[1,8,32]{2,1,0:T(8,128)S(1)}) fusion(f32[128,32]{1,0:T(8,128)} %copy-done.9, s32[]{:T(128)S(6)} %select_n.93, pred[]{:T(512)S(6)} %eq.7, f32[304,128]{1,0:T(8,128)} %collective-permute-done.2, s32[]{:T(128)S(6)} %select_n.95, pred[]{:T(512)S(6)} %eq.6, f32[8,4096]{1,0:T(8,128)S(1)} %reshape.149, ...), kind=kOutput, calls=%fused_computation.63 | convolution fusion | flops 6292224 | bytes 660490 | tf_op jit(solution)/shard_map/dot_general | solution.py:101
  90.4 0.7 fusion.15
  91.2 0.7 pad_maximum_fusion
  (53 shorter events, 1.1 us)
Async XLA Ops:
  0.0 10.5 %copy-start = (f32[32,4096]{1,0:T(8,128)S(1)}, f32[32,4096]{1,0:T(8,128)}, u32[]{:S(2)}) copy-start(f32[32,4096]{1,0:T(8,128)} %param.19) | copy-start | bytes 1572868
  0.0 11.1 %copy-start.2 = (f32[4,8,512]{2,1,0:T(8,128)S(1)}, f32[4,8,512]{2,1,0:T(8,128)}, u32[]{:S(2)}) copy-start(f32[4,8,512]{2,1,0:T(8,128)} %param.16) | copy-start | bytes 196612
  0.0 10.6 %copy-start.8 = (f32[1,32,128]{2,1,0:T(8,128)S(1)}, f32[1,32,128]{2,1,0:T(8,128)}, u32[]{:S(2)}) copy-start(f32[1,32,128]{2,1,0:T(8,128)} %param.18) | copy-start | bytes 49156
  1.0 10.4 %copy-start.1 = (bf16[4,512,512]{2,1,0:T(8,128)(2,1)S(1)}, bf16[4,512,512]{2,1,0:T(8,128)(2,1)}, u32[]{:S(2)}) copy-start(bf16[4,512,512]{2,1,0:T(8,128)(2,1)} %param.15) | copy-start | bytes 6291460
  1.0 10.0 %collective-permute-start.1 = (f32[1,32,128]{2,1,0:T(8,128)S(1)}, f32[1,32,128]{2,1,0:T(8,128)S(1)}, u32[]{:S(2)}, u32[]{:S(2)}) collective-permute-start(f32[1,32,128]{2,1,0:T(8,128)S(1)} %get-tuple-element.67), channel_id=1, source_target_pairs={{1,0},{2,1},{3,2},{4,3},{5,4},{6,5},{7,6},{8,7},{9,8},{10,9},{11,1... | collective-permute-start | bytes 49160 | tf_op jit(solution)/shard_map/ppermute | solution.py:13
  3.5 7.5 %collective-permute-start = (f32[1,32,128]{2,1,0:T(8,128)S(1)}, f32[1,32,128]{2,1,0:T(8,128)S(1)}, u32[]{:S(2)}, u32[]{:S(2)}) collective-permute-start(f32[1,32,128]{2,1,0:T(8,128)S(1)} %get-tuple-element.68), channel_id=1, source_target_pairs={{0,1},{1,2},{2,3},{3,4},{4,5},{5,6},{6,7},{7,8},{8,9},{9,10},{10,1... | collective-permute-start | bytes 49160 | tf_op jit(solution)/shard_map/ppermute | solution.py:13
  23.1 34.0 %copy-start.3 = (f32[128,32]{1,0:T(8,128)}, f32[128,32]{1,0:T(8,128)S(1)}, u32[]{:S(2)}) copy-start(f32[128,32]{1,0:T(8,128)S(1)} %convolution_bitcast_fusion.1) | copy-start | bytes 49156
  57.1 30.2 %collective-permute-start.2 = (f32[304,128]{1,0:T(8,128)}, f32[304,128]{1,0:T(8,128)}, u32[]{:S(2)}, u32[]{:S(2)}) collective-permute-start(f32[304,128]{1,0:T(8,128)} %select_maximum_fusion), channel_id=1, source_target_pairs={{3,4},{7,8},{11,12},{15,16},{19,20},{23,24},{27,28},{31,32},{35,36... | collective-permute-start | bytes 466952 | tf_op jit(solution)/shard_map/ppermute | solution.py:90
  84.2 1.8 %copy-start.4 = (f32[128,32]{1,0:T(8,128)S(1)}, f32[128,32]{1,0:T(8,128)}, u32[]{:S(2)}) copy-start(f32[128,32]{1,0:T(8,128)} %copy-done.3) | copy-start | bytes 49156
  84.2 2.1 %copy-start.5 = (f32[1,32,512]{2,1,0:T(8,128)S(1)}, f32[1,32,512]{2,1,0:T(8,128)}, u32[]{:S(2)}) copy-start(f32[1,32,512]{2,1,0:T(8,128)} %get-tuple-element.73) | copy-start | bytes 196612
  84.2 2.1 %copy-start.6 = (f32[1,32,512]{2,1,0:T(8,128)S(1)}, f32[1,32,512]{2,1,0:T(8,128)}, u32[]{:S(2)}) copy-start(f32[1,32,512]{2,1,0:T(8,128)} %get-tuple-element.74) | copy-start | bytes 196612
  86.3 1.0 %copy-start.9 = (f32[128,32]{1,0:T(8,128)}, f32[128,32]{1,0:T(8,128)S(1)}, u32[]{:S(2)}) copy-start(f32[128,32]{1,0:T(8,128)S(1)} %fusion) | copy-start | bytes 49156
  88.2 3.0 %copy-start.7 = (f32[3,32,128]{2,1,0:T(8,128)S(1)}, f32[3,32,128]{2,1,0:T(8,128)}, u32[]{:S(2)}) copy-start(f32[3,32,128]{2,1,0:T(8,128)} %get-tuple-element.64) | copy-start | bytes 147460

commit v12 on v10

--- a/solution.py
+++ b/solution.py
@@ -52,7 +52,10 @@
         "srk,sjk->srj", rhs_low[::residual_in.shape[0] - 1], local_inverse[::residual_in.shape[0] - 1],
         preferred_element_type=jnp.float32)
     local = jnp.concatenate([edge_local[:1], inner_local, edge_local[1:]], 0)
-    coarse = jnp.einsum("snk,srk->snr", coarse_basis, rhs, precision=high)
+    inner_coarse = jnp.einsum("snk,srk->snr", coarse_basis[1:-1], inner, precision=high)
+    edge_coarse = jnp.einsum(
+        "snk,srk->snr", coarse_basis[::residual_in.shape[0] - 1], rhs[::residual_in.shape[0] - 1], precision=high)
+    coarse = jnp.concatenate([edge_coarse[:1], inner_coarse, edge_coarse[1:]], 0)
     nrhs = local.shape[1]
 
     first_local = local[0, :, :IFW]

time: 83.1 us -> 83.3 us (level)
    dot_general x1 -> x2, matrix products: 0.23 us -> 1.07 us  [the longest x1 0.92 us: shards(): jnp.einsum('snk,srk->snr', coarse_basis[1:-1], inner, precision=high)]
  transfers between devices with their start and end apart: 3 -> 3, of which waited for: 0 -> 0; matrix products, arithmetic and copies ran while one was open for 4% -> 5% of each run, Pallas kernels for 0% -> 0%
where the time goes in v12:
time: 83.3 us; the launch traced here: 83 us
  blocking collectives  56.3 us (68%)
  starting transfers between devices  18.4 us (22%)
  matrix products  5.11 us (6%)
  local copies, waits for them, and re-layouts  1.77 us (2%)
  other arithmetic  1.05 us (1%)
    all_gather x2, blocking collectives, shards(): gathered_in = lax.all_gather(gathered_in, axis, axis=0, tiled=True)  34 us
    all_gather x1, blocking collectives, shards(): gathered_in = lax.all_gather(gathered_in, 'x', axis=0, tiled=True)  11.9 us
    all_gather x1, blocking collectives, shards(): gathered = lax.all_gather(packed, 'sub', axis=0, tiled=False)  10.4 us
    ppermute x1, starting transfers between devices, shards(): incoming = lax.ppermute(outgoing, SPREAD, pairs)  10.3 us
    ppermute x2, starting transfers between devices, from_behind_2(): return lax.ppermute(array, axis, pairs)  8.07 us
  transfers between devices with their start and end apart: 3, of which 0 were waited for; matrix products, arithmetic and copies ran while one was open for 5% of the time, Pallas kernels for 0%

profile of v12, /device:TPU:1, one launch (start us, length us, event | category | flops | bytes accessed | tf_op | source)
XLA Modules:
  0.0 83.0 jit_solution(6535124910172652679)
XLA Ops:
  0.0 1.0 %copy.33 = f32[4,32,512]{2,1,0:T(8,128)S(1)} copy(f32[4,32,512]{2,1,0:T(8,128)} %param.14) | data formatting | bytes 524288
  1.0 4.2 %collective-permute-start = (f32[1,32,128]{2,1,0:T(8,128)S(1)}, f32[1,32,128]{2,1,0:T(8,128)S(1)}, u32[]{:S(2)}, u32[]{:S(2)}) collective-permute-start(f32[1,32,128]{2,1,0:T(8,128)S(1)} %get-tuple-element.68), channel_id=1, source_target_pairs={{0,1},{1,2},{2,3},{3,4},{4,5},{5,6},{6,7},{7,8},{8,9},{9,10},{10,1... | collective-permute-start | bytes 49160 | tf_op jit(solution)/shard_map/ppermute | solution.py:13
  5.2 3.9 %collective-permute-start.1 = (f32[1,32,128]{2,1,0:T(8,128)S(1)}, f32[1,32,128]{2,1,0:T(8,128)S(1)}, u32[]{:S(2)}, u32[]{:S(2)}) collective-permute-start(f32[1,32,128]{2,1,0:T(8,128)S(1)} %get-tuple-element.67), channel_id=1, source_target_pairs={{1,0},{2,1},{3,2},{4,3},{5,4},{6,5},{7,6},{8,7},{9,8},{10,9},{11,1... | collective-permute-start | bytes 49160 | tf_op jit(solution)/shard_map/ppermute | solution.py:13
  9.2 0.9 %convolution_bitcast_fusion.3 = f32[2,8,32]{2,1,0:T(8,128)S(1)} fusion(f32[2,32,512]{2,1,0:T(8,128)S(1)} %fusion.12, f32[4,8,512]{2,1,0:T(8,128)} %param.16), kind=kOutput, calls=%fused_computation.5 | convolution fusion | flops 1572864 | bytes 165888 | tf_op jit(solution)/shard_map/snk,srk->snr/dot_general | solution.py:55
  10.1 1.6 %fusion.1 = f32[2,32,512]{2,1,0:T(8,128)S(1)} fusion(bf16[4,512,512]{2,1,0:T(8,128)(2,1)} %param.15, f32[2,32,512]{2,1,0:T(8,128)S(1)} %fusion.12), kind=kOutput, calls=%fused_computation.7 | convolution fusion | flops 33587200 | bytes 1310720 | tf_op jit(solution)/shard_map/srk,sjk->srj/dot_general | solution.py:49
  11.8 0.3 fusion.19
  12.3 0.2 convolution_bitcast_fusion.4
  12.6 0.4 fusion.3
  13.1 10.4 %all-gather = f32[352,128]{1,0:T(8,128)S(1)} all-gather(f32[88,128]{1,0:T(8,128)S(1)} %constant_dynamic-update-slice_fusion), channel_id=2, replica_groups=mesh['x'=4,'z'=16,'core'=2,'sub'=4] {'sub'}, dimensions={0}, use_global_device_ids=true | all-gather | bytes 225280 | tf_op jit(solution)/shard_map/all_gather | solution.py:70
  23.4 0.1 reshape.138
  23.5 0.2 convolution_bitcast_fusion.2
  23.8 5.9 %all_gather.17 = f32[64,32]{1,0:T(8,128)S(1)} all-gather(f32[32,32]{1,0:T(8,128)S(1)} %copy.18), channel_id=1, replica_groups=mesh['x'=4,'z'=16,'core'=2,'sub'=4] {'core'}, dimensions={0}, use_global_device_ids=true | all-gather | bytes 12288 | tf_op jit(solution)/shard_map/all_gather | solution.py:91
  29.8 28.1 %all-gather.1 = f32[16,64,32]{1,2,0:T(8,128)S(1)} all-gather(f32[1,64,32]{1,2,0:T(8,128)S(1)} %copy.19), channel_id=1, replica_groups=mesh['x'=4,'z'=16,'core'=2,'sub'=4] {'z'}, dimensions={0}, use_global_device_ids=true | all-gather | bytes 139264 | tf_op jit(solution)/shard_map/all_gather | solution.py:91
  57.9 0.2 copy.20
  58.0 0.1 reshape.144
  58.2 0.2 convolution_bitcast_fusion.1
  58.4 10.3 %collective-permute-start.2 = (f32[304,128]{1,0:T(8,128)S(1)}, f32[304,128]{1,0:T(8,128)S(1)}, u32[]{:S(2)}, u32[]{:S(2)}) collective-permute-start(f32[304,128]{1,0:T(8,128)S(1)} %select_maximum_fusion), channel_id=1, source_target_pairs={{3,4},{7,8},{11,12},{15,16},{19,20},{23,24},{27,28},{31,32},{35,36... | collective-permute-start | bytes 466952 | tf_op jit(solution)/shard_map/ppermute | solution.py:93
  68.7 11.9 %all_gather.19 = f32[4096,32]{0,1:T(8,128)S(1)} all-gather(f32[1024,32]{0,1:T(8,128)S(1)} %reshape.144), channel_id=1, replica_groups=mesh['x'=4,'z'=16,'core'=2,'sub'=4] {'x'}, dimensions={0}, use_global_device_ids=true | all-gather | bytes 655360 | tf_op jit(solution)/shard_map/all_gather | solution.py:94
  80.6 0.4 fusion.40
  81.0 0.2 fusion
  81.2 0.3 convolution_add_fusion
  81.7 0.3 select_bitcast_fusion.1
  82.1 0.1 multiply_reduce_fusion
  82.3 0.7 pad_maximum_fusion
  (47 shorter events, 0.6 us)
Async XLA Ops:
  0.0 11.7 %copy-start = (f32[32,4096]{1,0:T(8,128)S(1)}, f32[32,4096]{1,0:T(8,128)}, u32[]{:S(2)}) copy-start(f32[32,4096]{1,0:T(8,128)} %param.19) | copy-start | bytes 1572868
  0.0 12.3 %copy-start.2 = (f32[4,8,512]{2,1,0:T(8,128)S(1)}, f32[4,8,512]{2,1,0:T(8,128)}, u32[]{:S(2)}) copy-start(f32[4,8,512]{2,1,0:T(8,128)} %param.16) | copy-start | bytes 196612
  0.0 11.8 %copy-start.3 = (f32[1,32,128]{2,1,0:T(8,128)S(1)}, f32[1,32,128]{2,1,0:T(8,128)}, u32[]{:S(2)}) copy-start(f32[1,32,128]{2,1,0:T(8,128)} %param.18) | copy-start | bytes 49156
  1.0 11.6 %copy-start.1 = (bf16[4,512,512]{2,1,0:T(8,128)(2,1)S(1)}, bf16[4,512,512]{2,1,0:T(8,128)(2,1)}, u32[]{:S(2)}) copy-start(bf16[4,512,512]{2,1,0:T(8,128)(2,1)} %param.15) | copy-start | bytes 6291460
  1.0 11.2 %collective-permute-start = (f32[1,32,128]{2,1,0:T(8,128)S(1)}, f32[1,32,128]{2,1,0:T(8,128)S(1)}, u32[]{:S(2)}, u32[]{:S(2)}) collective-permute-start(f32[1,32,128]{2,1,0:T(8,128)S(1)} %get-tuple-element.68), channel_id=1, source_target_pairs={{0,1},{1,2},{2,3},{3,4},{4,5},{5,6},{6,7},{7,8},{8,9},{9,10},{10,1... | collective-permute-start | bytes 49160 | tf_op jit(solution)/shard_map/ppermute | solution.py:13
  5.2 7.0 %collective-permute-start.1 = (f32[1,32,128]{2,1,0:T(8,128)S(1)}, f32[1,32,128]{2,1,0:T(8,128)S(1)}, u32[]{:S(2)}, u32[]{:S(2)}) collective-permute-start(f32[1,32,128]{2,1,0:T(8,128)S(1)} %get-tuple-element.67), channel_id=1, source_target_pairs={{1,0},{2,1},{3,2},{4,3},{5,4},{6,5},{7,6},{8,7},{9,8},{10,9},{11,1... | collective-permute-start | bytes 49160 | tf_op jit(solution)/shard_map/ppermute | solution.py:13
  12.2 45.9 %copy-start.4 = (f32[1,128,128]{2,1,0:T(8,128)S(1)}, f32[1,128,128]{2,1,0:T(8,128)}, u32[]{:S(2)}) copy-start(f32[1,128,128]{2,1,0:T(8,128)} %param.17) | copy-start | bytes 196612
  58.4 23.2 %collective-permute-start.2 = (f32[304,128]{1,0:T(8,128)S(1)}, f32[304,128]{1,0:T(8,128)S(1)}, u32[]{:S(2)}, u32[]{:S(2)}) collective-permute-start(f32[304,128]{1,0:T(8,128)S(1)} %select_maximum_fusion), channel_id=1, source_target_pairs={{3,4},{7,8},{11,12},{15,16},{19,20},{23,24},{27,28},{31,32},{35,36... | collective-permute-start | bytes 466952 | tf_op jit(solution)/shard_map/ppermute | solution.py:93
